TPU v7x, 32 devices: a whole 2x2x4 slice. The times are simulated.
32 devices in a mesh: parts: 2 (over y), ctx: 8 (over z, x), tp: 2 (over core).
Axes of the slice: x: 2, y: 2, z: 4, core: 2. Of those that a mesh axis runs over, the one named last changes fastest.
Arguments:
- queries: bfloat16 [2048, 8192], P(('parts', 'ctx'), 'tp'), parts along dimension 0, may hold values from -9 to 9
- episode_key_cache: bfloat16 [128, 16, 1024], P(None, ('parts', 'ctx'), 'tp'), parts along dimension 1, may hold values from -9 to 9
- episode_value_cache: bfloat16 [128, 16, 1024], P(None, ('parts', 'ctx'), 'tp'), parts along dimension 1, may hold values from -6 to 6
- output_gradient: bfloat16 [2048, 8192], P(('parts', 'ctx'), 'tp'), parts along dimension 0, may hold values from -6 to 6
- block_lists: int32 [16, 2], P(('parts', 'ctx')), parts along dimension 0, may hold values from 0 to 7, as said below
- block_counts: int32 [16], P(('parts', 'ctx')), parts along dimension 0, may hold values from 1 to 2
Outputs:
- attn_out: bfloat16 [2048, 8192], P(('parts', 'ctx'), 'tp'), parts along dimension 0
- query_grad: bfloat16 [2048, 8192], P(('parts', 'ctx'), 'tp'), parts along dimension 0
- key_cache_gradient: bfloat16 [128, 16, 1024], P(None, ('parts', 'ctx'), 'tp'), parts along dimension 1
- value_cache_gradient: bfloat16 [128, 16, 1024], P(None, ('parts', 'ctx'), 'tp'), parts along dimension 1
There are 2 independent parts, one for each index of `parts`. A program takes and returns all parts, laid end to end along the dimension named above; each array names one. Nothing has to cross between parts.
Inputs may be any that keep to these rules, and one draw needn't show every extreme that they name: `block_lists`: each row names 2 different key blocks; a query block reads only its first block_counts entries.
All inputs are finite; a program needn't handle non-finite values.
Results may differ from a plain program's by a relative error of at most 0.0085.
The roundings to bfloat16 on the way count: a program that leaves them out, or rounds other values in their place, can miss the bound.
Values may be sent and summed in bfloat16 or wider, within the bound.
No kernel may reach another device: no remote copies, remote signals or barrier semaphores. Data moves between devices by JAX's collectives and lax.ppermute only.
A program may use at most 64 MiB of HBM per device.

v0:
```python
import jax
import jax.numpy as jnp
from jax import lax
from jax.sharding import PartitionSpec as P

QUERY_HEADS = 64
KEY_VALUE_HEADS = 8
HEAD_SIZE = 128
LIST = 2


def attend_group(query_part, key_part, value_part, grad_part, live_slots):
    score_scale = HEAD_SIZE ** (-0.5)
    scores = score_scale * jnp.einsum(
        "qah,jkh->aqjk", query_part, key_part, preferred_element_type=jnp.float32
    )
    masked = jnp.where(live_slots[None, None, :, None], scores, -jnp.inf)
    row_peak = jnp.max(masked, axis=(2, 3), keepdims=True)
    exponent = jnp.exp(masked - row_peak)
    weights = exponent / jnp.sum(exponent, axis=(2, 3), keepdims=True)
    weights_low = weights.astype(jnp.bfloat16)
    attended = jnp.einsum(
        "aqjk,jkh->qah", weights_low, value_part, preferred_element_type=jnp.float32
    ).astype(jnp.bfloat16)
    attended = lax.optimization_barrier(attended)
    row_delta = jnp.sum(grad_part.astype(jnp.float32) * attended.astype(jnp.float32), axis=2)
    weight_grad = jnp.einsum(
        "qah,jkh->aqjk", grad_part, value_part, preferred_element_type=jnp.float32
    )
    score_grad = (weights * (weight_grad - row_delta.T[:, :, None, None])).astype(jnp.bfloat16)
    query_grad = (
        score_scale
        * jnp.einsum("aqjk,jkh->qah", score_grad, key_part, preferred_element_type=jnp.float32)
    ).astype(jnp.bfloat16)
    key_piece = score_scale * jnp.einsum(
        "aqjk,qah->jkh", score_grad, query_part, preferred_element_type=jnp.float32
    )
    value_piece = jnp.einsum(
        "aqjk,qah->jkh", weights_low, grad_part, preferred_element_type=jnp.float32
    )
    return (attended, query_grad, key_piece, value_piece)


def arrange_rows(arrived):
    row_count, slot_count, peer_count, column_count = arrived.shape
    return jnp.transpose(arrived, (1, 2, 0, 3)).reshape(
        slot_count, peer_count * row_count, column_count
    )


def split_rows(pieces, row_count):
    slot_count, row_total, column_count = pieces.shape
    shaped = pieces.reshape(slot_count, row_total // row_count, row_count, column_count)
    return jnp.transpose(shaped, (2, 0, 1, 3))


def owner_sum(arrived, selector):
    summed = jnp.einsum("rjpc,jpn->rnc", arrived, selector, precision=lax.Precision.HIGHEST)
    return summed.astype(jnp.bfloat16)


def shards(
    queries, episode_key_cache, episode_value_cache, output_gradient, block_lists, block_counts
):
    held_keys, held_values = (
        lax.all_to_all(episode_key_cache, "ctx", split_axis=0, concat_axis=1, tiled=True),
        lax.all_to_all(episode_value_cache, "ctx", split_axis=0, concat_axis=1, tiled=True),
    )
    row_count = held_keys.shape[0]
    block_total = held_keys.shape[1]
    local_groups = held_keys.shape[2] // HEAD_SIZE
    queries_per_group = QUERY_HEADS // KEY_VALUE_HEADS
    query_rows = queries.shape[0]
    listed_all = lax.all_gather(block_lists, "ctx", axis=0, tiled=True)
    wanted = listed_all.T
    live_slots = jnp.arange(LIST, dtype=jnp.int32) < block_counts[0]
    selector = (
        wanted[:, :, None] == jnp.arange(block_total, dtype=jnp.int32)[None, None, :]
    ).astype(jnp.float32)
    picked_keys = jnp.take(held_keys, wanted, axis=1)
    picked_values = jnp.take(held_values, wanted, axis=1)

    def run_group(group_index, key_rows, value_rows):
        first_col = group_index * queries_per_group * HEAD_SIZE
        last_col = first_col + queries_per_group * HEAD_SIZE
        query_part = queries[:, first_col:last_col].reshape(
            query_rows, queries_per_group, HEAD_SIZE
        )
        grad_part = output_gradient[:, first_col:last_col].reshape(
            query_rows, queries_per_group, HEAD_SIZE
        )
        return attend_group(query_part, key_rows, value_rows, grad_part, live_slots)

    arrived_keys, arrived_values = (
        lax.all_to_all(picked_keys, "ctx", split_axis=2, concat_axis=2, tiled=True),
        lax.all_to_all(picked_values, "ctx", split_axis=2, concat_axis=2, tiled=True),
    )
    fetched_keys = arrange_rows(arrived_keys)
    fetched_values = arrange_rows(arrived_values)
    results = [
        run_group(
            group_index,
            fetched_keys[:, :, group_index * HEAD_SIZE : (group_index + 1) * HEAD_SIZE],
            fetched_values[:, :, group_index * HEAD_SIZE : (group_index + 1) * HEAD_SIZE],
        )
        for group_index in range(local_groups)
    ]
    key_pieces = jnp.concatenate([outcome[2] for outcome in results], axis=2)
    value_pieces = jnp.concatenate([outcome[3] for outcome in results], axis=2)
    back_keys, back_values = (
        lax.all_to_all(
            split_rows(key_pieces, row_count).astype(jnp.bfloat16),
            "ctx",
            split_axis=2,
            concat_axis=2,
            tiled=True,
        ).astype(jnp.float32),
        lax.all_to_all(
            split_rows(value_pieces, row_count).astype(jnp.bfloat16),
            "ctx",
            split_axis=2,
            concat_axis=2,
            tiled=True,
        ).astype(jnp.float32),
    )
    row_key_grad = owner_sum(back_keys, selector)
    row_value_grad = owner_sum(back_values, selector)
    key_cache_gradient, value_cache_gradient = (
        lax.all_to_all(row_key_grad, "ctx", split_axis=1, concat_axis=0, tiled=True),
        lax.all_to_all(row_value_grad, "ctx", split_axis=1, concat_axis=0, tiled=True),
    )
    attn_out = jnp.concatenate(
        [outcome[0].reshape(query_rows, queries_per_group * HEAD_SIZE) for outcome in results],
        axis=1,
    )
    query_grad = jnp.concatenate(
        [outcome[1].reshape(query_rows, queries_per_group * HEAD_SIZE) for outcome in results],
        axis=1,
    )
    return (attn_out, query_grad, key_cache_gradient, value_cache_gradient)


def solution(mesh):
    placed = (
        P(("parts", "ctx"), "tp"),
        P(None, ("parts", "ctx"), "tp"),
        P(None, ("parts", "ctx"), "tp"),
        P(("parts", "ctx"), "tp"),
        P(("parts", "ctx"), None),
        P(("parts", "ctx")),
    )
    return jax.shard_map(
        shards,
        mesh=mesh,
        in_specs=placed,
        out_specs=(
            P(("parts", "ctx"), "tp"),
            P(("parts", "ctx"), "tp"),
            P(None, ("parts", "ctx"), "tp"),
            P(None, ("parts", "ctx"), "tp"),
        ),
        check_vma=False,
    )
```

profile of v0, /device:TPU:0, one launch (start us, length us, event | category | flops | bytes accessed | tf_op | source)
XLA Modules:
  0.0 133.8 jit_solution(3935929716690283083)
XLA Ops:
  1.1 1.6 %reduce = bf16[128,512]{1,0:T(8,128)(2,1)S(1)} reduce(bf16[128,1,512]{2,0,1:T(8,128)(2,1)} %param.10, bf16[]{:T(256)} %broadcast.110), dimensions={1}, to_apply=%copy.184.reduce_sub_computation | reduce | bytes 262146 | tf_op args[2]
  3.5 7.3 %all-to-all-start = ((bf16[8,2,4096]{2,1,0:T(2,128)(2,1)}), bf16[8,2,4096]{2,1,0:T(2,128)(2,1)S(1)}, u32[]{:S(2)}, u32[]{:S(2)}) async-start(bf16[8,2,4096]{2,1,0:T(2,128)(2,1)} %reshape.189), calls=%async_computation | async-start | bytes 262144 | tf_op jit(solution)/shard_map/all_to_all | solution.py:67
  10.7 21.1 %all-gather = s32[8,1,2]{2,1,0:T(1,128)S(1)} all-gather(s32[1,1,2]{2,1,0:T(1,128)} %bitcast.467), channel_id=1, replica_groups=mesh['parts'=2,'ctx'=8,'tp'=2] {'ctx'}, dimensions={0}, use_global_device_ids=true | all-gather | bytes 72 | tf_op jit(solution)/shard_map/all_gather | solution.py:74
  32.1 1.6 %reduce.1 = bf16[128,512]{1,0:T(8,128)(2,1)S(1)} reduce(bf16[128,1,512]{2,0,1:T(8,128)(2,1)} %param.9, bf16[]{:T(256)} %broadcast.110), dimensions={1}, to_apply=%copy.188.reduce_sub_computation | reduce | bytes 262146 | tf_op args[1]
  34.4 3.4 %all-to-all-start.2 = ((bf16[8,2,4096]{2,1,0:T(2,128)(2,1)}), bf16[8,2,4096]{2,1,0:T(2,128)(2,1)S(1)}, u32[]{:S(2)}, u32[]{:S(2)}) async-start(bf16[8,2,4096]{2,1,0:T(2,128)(2,1)} %reshape.187), calls=%async_computation.2 | async-start | bytes 262144 | tf_op jit(solution)/shard_map/all_to_all | solution.py:66
  37.9 7.1 %all-to-all-done.2 = bf16[8,2,4096]{2,1,0:T(2,128)(2,1)S(1)} async-done(((bf16[8,2,4096]{2,1,0:T(2,128)(2,1)}), bf16[8,2,4096]{2,1,0:T(2,128)(2,1)S(1)}, u32[]{:S(2)}, u32[]{:S(2)}) %all-to-all-start.2) | async-done | bytes 131104 | tf_op jit(solution)/shard_map/all_to_all | solution.py:66
  47.2 3.4 %all-to-all-start.3 = ((bf16[16,2,8,512]{3,0,1,2:T(8,128)(2,1)}), bf16[16,2,8,512]{3,0,1,2:T(8,128)(2,1)S(1)}, u32[]{:S(2)}, u32[]{:S(2)}) async-start(bf16[16,2,8,512]{3,0,1,2:T(8,128)(2,1)} %copy.189), calls=%async_computation.3 | async-start | bytes 524288 | tf_op jit(solution)/shard_map/all_to_all | solution.py:95
  52.6 0.9 fusion.71
  53.5 1.2 copy.210
  56.6 2.2 %all-to-all-done.3 = bf16[16,2,8,512]{3,0,1,2:T(8,128)(2,1)S(1)} async-done(((bf16[16,2,8,512]{3,0,1,2:T(8,128)(2,1)}), bf16[16,2,8,512]{3,0,1,2:T(8,128)(2,1)S(1)}, u32[]{:S(2)}, u32[]{:S(2)}) %all-to-all-start.3) | async-done | bytes 262176 | tf_op jit(solution)/shard_map/all_to_all | solution.py:95
  58.8 4.0 %all-to-all-start.1 = ((bf16[16,2,8,512]{3,0,1,2:T(8,128)(2,1)}), bf16[16,2,8,512]{3,0,1,2:T(8,128)(2,1)}, u32[]{:S(2)}, u32[]{:S(2)}) async-start(bf16[16,2,8,512]{3,0,1,2:T(8,128)(2,1)} %copy.185), calls=%async_computation.1 | async-start | bytes 524288 | tf_op jit(solution)/shard_map/all_to_all | solution.py:96
  64.2 6.8 %all-to-all-done.1 = bf16[16,2,8,512]{3,0,1,2:T(8,128)(2,1)} async-done(((bf16[16,2,8,512]{3,0,1,2:T(8,128)(2,1)}), bf16[16,2,8,512]{3,0,1,2:T(8,128)(2,1)}, u32[]{:S(2)}, u32[]{:S(2)}) %all-to-all-start.1) | async-done | bytes 262176 | tf_op jit(solution)/shard_map/all_to_all | solution.py:96
  71.1 1.0 copy.186
  73.4 1.0 fusion.28
  76.8 0.9 fusion.30
  78.7 0.9 fusion.50
  83.1 2.0 %copy.239 = bf16[16,2,8,512]{3,1,0,2:T(2,128)(2,1)} copy(bf16[16,2,8,512]{3,0,2,1:T(8,128)(2,1)} %bitcast.447) | data formatting | bytes 524288 | tf_op jit(solution)/shard_map/convert_element_type | solution.py:112
  85.0 4.0 %all-to-all-start.4 = ((bf16[16,2,8,512]{3,1,0,2:T(2,128)(2,1)}), bf16[16,2,8,512]{3,1,0,2:T(2,128)(2,1)}, u32[]{:S(2)}, u32[]{:S(2)}) async-start(bf16[16,2,8,512]{3,1,0,2:T(2,128)(2,1)} %copy.239), calls=%async_computation.4 | async-start | bytes 524288 | tf_op jit(solution)/shard_map/all_to_all | solution.py:111
  89.1 1.0 fusion.29
  90.4 1.1 copy.231
  91.6 1.1 copy.232
  93.9 0.9 pad_maximum_fusion.3
  94.9 1.0 copy.247
  95.9 1.5 %all-to-all-done.4 = bf16[16,2,8,512]{3,1,0,2:T(2,128)(2,1)} async-done(((bf16[16,2,8,512]{3,1,0,2:T(2,128)(2,1)}), bf16[16,2,8,512]{3,1,0,2:T(2,128)(2,1)}, u32[]{:S(2)}, u32[]{:S(2)}) %all-to-all-start.4) | async-done | bytes 262176 | tf_op jit(solution)/shard_map/all_to_all | solution.py:111
  97.3 4.4 %all-to-all-start.6 = ((bf16[16,2,8,512]{3,1,0,2:T(2,128)(2,1)}), bf16[16,2,8,512]{3,1,0,2:T(2,128)(2,1)S(1)}, u32[]{:S(2)}, u32[]{:S(2)}) async-start(bf16[16,2,8,512]{3,1,0,2:T(2,128)(2,1)} %copy.247), calls=%async_computation.6 | async-start | bytes 524288 | tf_op jit(solution)/shard_map/all_to_all | solution.py:118
  102.3 1.2 fusion.39
  104.3 6.1 %all-to-all-done.6 = bf16[16,2,8,512]{3,1,0,2:T(2,128)(2,1)S(1)} async-done(((bf16[16,2,8,512]{3,1,0,2:T(2,128)(2,1)}), bf16[16,2,8,512]{3,1,0,2:T(2,128)(2,1)S(1)}, u32[]{:S(2)}, u32[]{:S(2)}) %all-to-all-start.6) | async-done | bytes 262176 | tf_op jit(solution)/shard_map/all_to_all | solution.py:118
  110.4 3.8 %all-to-all-start.5 = ((bf16[16,8,512]{2,0,1:T(8,128)(2,1)}), bf16[16,8,512]{2,0,1:T(8,128)(2,1)S(1)}, u32[]{:S(2)}, u32[]{:S(2)}) async-start(bf16[16,8,512]{2,0,1:T(8,128)(2,1)} %copy.241), calls=%async_computation.5 | async-start | bytes 262144 | tf_op jit(solution)/shard_map/all_to_all | solution.py:129
  115.2 6.5 %all-to-all-done.5 = bf16[16,8,512]{2,0,1:T(8,128)(2,1)S(1)} async-done(((bf16[16,8,512]{2,0,1:T(8,128)(2,1)}), bf16[16,8,512]{2,0,1:T(8,128)(2,1)S(1)}, u32[]{:S(2)}, u32[]{:S(2)}) %all-to-all-start.5) | async-done | bytes 131104 | tf_op jit(solution)/shard_map/all_to_all | solution.py:129
  121.8 3.4 %all-to-all-start.7 = ((bf16[16,8,512]{2,0,1:T(8,128)(2,1)}), bf16[16,8,512]{2,0,1:T(8,128)(2,1)S(1)}, u32[]{:S(2)}, u32[]{:S(2)}) async-start(bf16[16,8,512]{2,0,1:T(8,128)(2,1)} %copy.249), calls=%async_computation.7 | async-start | bytes 262144 | tf_op jit(solution)/shard_map/all_to_all | solution.py:130
  125.2 1.5 %pad_maximum_fusion = (bf16[128,4096]{1,0:T(8,128)(2,1)}, bf16[128,4096]{1,0:T(8,128)(2,1)}) fusion(bf16[128,1024]{1,0:T(8,128)(2,1)S(1)} %copy.209, bf16[128,1024]{1,0:T(8,128)(2,1)S(1)} %copy-done.7, bf16[128,1024]{1,0:T(8,128)(2,1)S(1)} %copy.207, bf16[128,1024]{1,0:T(8,128)(2,1)S(1)} %copy.206, bf16[128,1024]{1,0:T(8,128)(2,1)S(1)} %copy.233, ...), kind=kLoop, calls=%fused_computation.80 | loop fusion | flops 8388608 | bytes 4194304 | tf_op jit(solution)/shard_map/concatenate | solution.py:132
  126.7 5.8 %all-to-all-done.7 = bf16[16,8,512]{2,0,1:T(8,128)(2,1)S(1)} async-done(((bf16[16,8,512]{2,0,1:T(8,128)(2,1)}), bf16[16,8,512]{2,0,1:T(8,128)(2,1)S(1)}, u32[]{:S(2)}, u32[]{:S(2)}) %all-to-all-start.7) | async-done | bytes 131104 | tf_op jit(solution)/shard_map/all_to_all | solution.py:130
  (98 shorter events, 22.1 us)
Async XLA Ops:
  3.5 30.9 %all-to-all-start = ((bf16[8,2,4096]{2,1,0:T(2,128)(2,1)}), bf16[8,2,4096]{2,1,0:T(2,128)(2,1)S(1)}, u32[]{:S(2)}, u32[]{:S(2)}) async-start(bf16[8,2,4096]{2,1,0:T(2,128)(2,1)} %reshape.189), calls=%async_computation | async-start | bytes 262144 | tf_op jit(solution)/shard_map/all_to_all | solution.py:67
  34.4 10.7 %all-to-all-start.2 = ((bf16[8,2,4096]{2,1,0:T(2,128)(2,1)}), bf16[8,2,4096]{2,1,0:T(2,128)(2,1)S(1)}, u32[]{:S(2)}, u32[]{:S(2)}) async-start(bf16[8,2,4096]{2,1,0:T(2,128)(2,1)} %reshape.187), calls=%async_computation.2 | async-start | bytes 262144 | tf_op jit(solution)/shard_map/all_to_all | solution.py:66
  46.3 4.3 %copy-start.8 = (bf16[128,4096]{1,0:T(8,128)(2,1)S(1)}, bf16[128,4096]{1,0:T(8,128)(2,1)}, u32[]{:S(2)}) copy-start(bf16[128,4096]{1,0:T(8,128)(2,1)} %param.8) | copy-start | bytes 3145732
  47.2 11.6 %all-to-all-start.3 = ((bf16[16,2,8,512]{3,0,1,2:T(8,128)(2,1)}), bf16[16,2,8,512]{3,0,1,2:T(8,128)(2,1)S(1)}, u32[]{:S(2)}, u32[]{:S(2)}) async-start(bf16[16,2,8,512]{3,0,1,2:T(8,128)(2,1)} %copy.189), calls=%async_computation.3 | async-start | bytes 524288 | tf_op jit(solution)/shard_map/all_to_all | solution.py:95
  51.4 1.2 copy-start.9
  53.5 2.2 %copy-start.11 = (bf16[128,1024]{1,0:T(8,128)(2,1)S(1)}, bf16[128,1024]{1,0:T(8,128)(2,1)}, u32[]{:S(2)}) copy-start(bf16[128,1024]{1,0:T(8,128)(2,1)} %get-tuple-element.8) | copy-start | bytes 786436
  55.7 8.3 %copy-start.1 = (bf16[128,1024]{0,1:T(8,128)(2,1)}, bf16[128,1024]{0,1:T(8,128)(2,1)S(1)}, u32[]{:S(2)}) copy-start(bf16[128,1024]{0,1:T(8,128)(2,1)S(1)} %copy.225) | copy-start | bytes 786436
  58.8 12.3 %all-to-all-start.1 = ((bf16[16,2,8,512]{3,0,1,2:T(8,128)(2,1)}), bf16[16,2,8,512]{3,0,1,2:T(8,128)(2,1)}, u32[]{:S(2)}, u32[]{:S(2)}) async-start(bf16[16,2,8,512]{3,0,1,2:T(8,128)(2,1)} %copy.185), calls=%async_computation.1 | async-start | bytes 524288 | tf_op jit(solution)/shard_map/all_to_all | solution.py:96
  62.8 0.7 copy-start.3
  71.1 1.3 copy-start.2
  72.4 1.0 copy-start.4
  74.8 1.0 copy-start
  80.0 0.8 copy-start.5
  82.2 6.9 %copy-start.6 = (bf16[8,128,2,128]{1,3,0,2:T(8,128)(2,1)S(1)}, bf16[8,128,2,128]{1,3,0,2:T(8,128)(2,1)}, u32[]{:S(2)}) copy-start(bf16[8,128,2,128]{1,3,0,2:T(8,128)(2,1)} %copy-done.5) | copy-start | bytes 1572868
  83.1 7.0 %copy-start.10 = (bf16[128,8,128]{2,0,1:T(8,128)(2,1)S(1)}, bf16[128,8,128]{2,0,1:T(8,128)(2,1)}, u32[]{:S(2)}) copy-start(bf16[128,8,128]{2,0,1:T(8,128)(2,1)} %fusion.28) | copy-start | bytes 786436
  85.0 12.3 %all-to-all-start.4 = ((bf16[16,2,8,512]{3,1,0,2:T(2,128)(2,1)}), bf16[16,2,8,512]{3,1,0,2:T(2,128)(2,1)}, u32[]{:S(2)}, u32[]{:S(2)}) async-start(bf16[16,2,8,512]{3,1,0,2:T(2,128)(2,1)} %copy.239), calls=%async_computation.4 | async-start | bytes 524288 | tf_op jit(solution)/shard_map/all_to_all | solution.py:111
  97.3 13.1 %all-to-all-start.6 = ((bf16[16,2,8,512]{3,1,0,2:T(2,128)(2,1)}), bf16[16,2,8,512]{3,1,0,2:T(2,128)(2,1)S(1)}, u32[]{:S(2)}, u32[]{:S(2)}) async-start(bf16[16,2,8,512]{3,1,0,2:T(2,128)(2,1)} %copy.247), calls=%async_computation.6 | async-start | bytes 524288 | tf_op jit(solution)/shard_map/all_to_all | solution.py:118
  102.3 22.8 %copy-start.7 = (bf16[128,1024]{1,0:T(8,128)(2,1)S(1)}, bf16[128,1024]{1,0:T(8,128)(2,1)}, u32[]{:S(2)}) copy-start(bf16[128,1024]{1,0:T(8,128)(2,1)} %copy.208) | copy-start | bytes 786436
  110.4 11.3 %all-to-all-start.5 = ((bf16[16,8,512]{2,0,1:T(8,128)(2,1)}), bf16[16,8,512]{2,0,1:T(8,128)(2,1)S(1)}, u32[]{:S(2)}, u32[]{:S(2)}) async-start(bf16[16,8,512]{2,0,1:T(8,128)(2,1)} %copy.241), calls=%async_computation.5 | async-start | bytes 262144 | tf_op jit(solution)/shard_map/all_to_all | solution.py:129
  121.8 10.7 %all-to-all-start.7 = ((bf16[16,8,512]{2,0,1:T(8,128)(2,1)}), bf16[16,8,512]{2,0,1:T(8,128)(2,1)S(1)}, u32[]{:S(2)}, u32[]{:S(2)}) async-start(bf16[16,8,512]{2,0,1:T(8,128)(2,1)} %copy.249), calls=%async_computation.7 | async-start | bytes 262144 | tf_op jit(solution)/shard_map/all_to_all | solution.py:130
where the time goes:
time: 135 us; the launch traced here: 134 us
  waiting for transfers between devices  36 us (27%)
  starting transfers between devices  33.8 us (25%)
  local copies, waits for them, and re-layouts  22.3 us (17%)
  blocking collectives  21.1 us (16%)
  matrix products  11.2 us (8%)
  other arithmetic  7.34 us (5%)
  between operations  1.9 us (1%)
    all_gather x1, blocking collectives, shards(): listed_all = lax.all_gather(block_lists, 'ctx', axis=0, tiled=True)  21.1 us
    all_to_all x1, starting transfers between devices, shards(): lax.all_to_all(episode_value_cache, 'ctx', split_axis=0, concat_axis=1, t...  7.28 us
    all_to_all x1, waiting for transfers between devices, shards(): lax.all_to_all(episode_key_cache, 'ctx', split_axis=0, concat_axis=1, til...  7.1 us
    all_to_all x1, waiting for transfers between devices, shards(): lax.all_to_all(picked_values, 'ctx', split_axis=2, concat_axis=2, tiled=T...  6.83 us
    all_to_all x1, waiting for transfers between devices, shards(): lax.all_to_all(row_key_grad, 'ctx', split_axis=1, concat_axis=0, tiled=True)  6.53 us
    unnamed x37, local copies, waits for them, and re-layouts  6.16 us
    all_to_all x1, waiting for transfers between devices, shards(): lax.all_to_all(split_rows(value_pieces, row_count).astype(jnp.bfloat16),...  6.15 us
    all_to_all x1, waiting for transfers between devices, shards(): lax.all_to_all(row_value_grad, 'ctx', split_axis=1, concat_axis=0, tiled=...  5.78 us
  transfers between devices with their start and end apart: 8, of which 7 were waited for; matrix products, arithmetic and copies ran while one was open for 15% of the time, Pallas kernels for 0%

commit v1 on v0

v1 whole, which is shorter than its diff:
```python
import jax
import jax.numpy as jnp
from jax import lax
from jax.sharding import PartitionSpec as P

QUERY_HEADS = 64
KEY_VALUE_HEADS = 8
HEAD_SIZE = 128
LIST = 2
TAG_COLUMNS = 128


def attend(query_part, key_part, value_part, grad_part, live_slots):
    score_scale = HEAD_SIZE ** (-0.5)
    scores = score_scale * jnp.einsum(
        "qgah,jkgh->gaqjk", query_part, key_part, preferred_element_type=jnp.float32
    )
    masked = jnp.where(live_slots[None, None, None, :, None], scores, -jnp.inf)
    row_peak = jnp.max(masked, axis=(3, 4), keepdims=True)
    exponent = jnp.exp(masked - row_peak)
    weights = exponent / jnp.sum(exponent, axis=(3, 4), keepdims=True)
    weights_low = weights.astype(jnp.bfloat16)
    attended = jnp.einsum(
        "gaqjk,jkgh->qgah", weights_low, value_part, preferred_element_type=jnp.float32
    ).astype(jnp.bfloat16)
    attended = lax.optimization_barrier(attended)
    row_delta = jnp.sum(grad_part.astype(jnp.float32) * attended.astype(jnp.float32), axis=3)
    weight_grad = jnp.einsum(
        "qgah,jkgh->gaqjk", grad_part, value_part, preferred_element_type=jnp.float32
    )
    score_grad = (
        weights * (weight_grad - jnp.transpose(row_delta, (1, 2, 0))[:, :, :, None, None])
    ).astype(jnp.bfloat16)
    query_grad = (
        score_scale
        * jnp.einsum("gaqjk,jkgh->qgah", score_grad, key_part, preferred_element_type=jnp.float32)
    ).astype(jnp.bfloat16)
    key_piece = score_scale * jnp.einsum(
        "gaqjk,qgah->jkgh", score_grad, query_part, preferred_element_type=jnp.float32
    )
    value_piece = jnp.einsum(
        "gaqjk,qgah->jkgh", weights_low, grad_part, preferred_element_type=jnp.float32
    )
    return attended, query_grad, key_piece, value_piece


def make_shards(peers):
    def shards(
        queries, episode_key_cache, episode_value_cache, output_gradient, block_lists, block_counts
    ):
        row_count = episode_key_cache.shape[0]
        key_width = episode_key_cache.shape[2]
        both_width = 2 * key_width
        chunk_rows = row_count // peers
        local_groups = key_width // HEAD_SIZE
        queries_per_group = QUERY_HEADS // KEY_VALUE_HEADS
        query_rows = queries.shape[0]

        held = jnp.concatenate(
            [episode_key_cache[:, 0, :], episode_value_cache[:, 0, :]], axis=1
        )
        tag = jnp.concatenate([block_lists[0], block_counts]).astype(jnp.bfloat16)
        tag_block = jnp.zeros((row_count, TAG_COLUMNS), jnp.bfloat16)
        tag_block = tag_block.at[:, : LIST + 1].set(jnp.broadcast_to(tag, (row_count, LIST + 1)))
        first_send = jnp.concatenate([held, tag_block], axis=1).reshape(
            peers, chunk_rows, both_width + TAG_COLUMNS
        )
        first_recv = lax.all_to_all(first_send, "ctx", 0, 0, tiled=True)
        info = first_recv[:, 0, both_width : both_width + LIST + 1].astype(jnp.int32)
        lists_all = info[:, :LIST]
        counts_all = info[:, LIST]

        rows_held = first_recv[:, :, :both_width]
        picked = jnp.take(rows_held, lists_all, axis=0, mode="clip")
        fetched = lax.all_to_all(picked, "ctx", 0, 2, tiled=True)[0]
        key_rows = fetched[:, :, :key_width].reshape(LIST, row_count, local_groups, HEAD_SIZE)
        value_rows = fetched[:, :, key_width:].reshape(LIST, row_count, local_groups, HEAD_SIZE)

        live_slots = jnp.arange(LIST, dtype=jnp.int32) < block_counts[0]
        query_part = queries.reshape(query_rows, local_groups, queries_per_group, HEAD_SIZE)
        grad_part = output_gradient.reshape(query_rows, local_groups, queries_per_group, HEAD_SIZE)
        attended, query_grad, key_piece, value_piece = attend(
            query_part, key_rows, value_rows, grad_part, live_slots
        )

        pieces = jnp.concatenate(
            [
                key_piece.reshape(LIST, row_count, key_width),
                value_piece.reshape(LIST, row_count, key_width),
            ],
            axis=2,
        ).astype(jnp.bfloat16)
        back = lax.all_to_all(
            pieces.reshape(LIST, peers, chunk_rows, both_width), "ctx", 1, 1, tiled=True
        )
        slot_live = jnp.arange(LIST, dtype=jnp.int32)[None, :] < counts_all[:, None]
        selector = (
            (lists_all[:, :, None] == jnp.arange(peers, dtype=jnp.int32)[None, None, :])
            & slot_live[:, :, None]
        ).astype(jnp.bfloat16)
        summed = jnp.einsum(
            "jqrc,qjn->nrc", back, selector, preferred_element_type=jnp.float32
        ).astype(jnp.bfloat16)

        owned = lax.all_to_all(summed, "ctx", 0, 0, tiled=True).reshape(row_count, both_width)
        key_cache_gradient = owned[:, None, :key_width]
        value_cache_gradient = owned[:, None, key_width:]
        attn_out = attended.reshape(query_rows, local_groups * queries_per_group * HEAD_SIZE)
        query_grad = query_grad.reshape(query_rows, local_groups * queries_per_group * HEAD_SIZE)
        return attn_out, query_grad, key_cache_gradient, value_cache_gradient

    return shards


def solution(mesh):
    placed = (
        P(("parts", "ctx"), "tp"),
        P(None, ("parts", "ctx"), "tp"),
        P(None, ("parts", "ctx"), "tp"),
        P(("parts", "ctx"), "tp"),
        P(("parts", "ctx"), None),
        P(("parts", "ctx")),
    )
    return jax.shard_map(
        make_shards(mesh.shape["ctx"]),
        mesh=mesh,
        in_specs=placed,
        out_specs=(
            P(("parts", "ctx"), "tp"),
            P(("parts", "ctx"), "tp"),
            P(None, ("parts", "ctx"), "tp"),
            P(None, ("parts", "ctx"), "tp"),
        ),
        check_vma=False,
    )
```

time: 135 us -> 89.1 us (0.66)
  starting transfers between devices: 33.8 us -> 10.8 us
  local copies, waits for them, and re-layouts: 22.3 us -> 13.9 us
  waiting for transfers between devices: 36 us -> 29.9 us
  blocking collectives: 21.1 us -> 17.4 us
  other arithmetic: 7.34 us -> 5.54 us
  matrix products: 11.2 us -> 9.43 us
    all_to_all x8 -> x3, starting transfers between devices: 33.8 us -> 10.8 us  [the longest x1 3.64 us: shards(): lax.all_to_all(pieces.reshape(LIST, peers, chunk_rows, both_width), 'ctx'...]
    all_gather x1 -> x0, blocking collectives: 21.1 us -> none  [shards(): listed_all = lax.all_gather(block_lists, 'ctx', axis=0, tiled=True)]
    all_to_all x0 -> x1, blocking collectives: none -> 17.4 us  [shards(): first_recv = lax.all_to_all(first_send, 'ctx', 0, 0, tiled=True)]
    all_to_all x8 -> x3, waiting for transfers between devices: 36 us -> 29.9 us  [the longest x1 14.2 us: shards(): lax.all_to_all(pieces.reshape(LIST, peers, chunk_rows, both_width), 'ctx'...]
    reshape x8 -> x0, local copies, waits for them, and re-layouts: 3.75 us -> none  [the longest x4 2.46 us: shards(): outcome[1].reshape(query_rows, queries_per_group * HEAD_SIZE)]
    convert_element_type x4 -> x1, local copies, waits for them, and re-layouts: 4.34 us -> 0.88 us  [shards(): summed = jnp.einsum('jqrc,qjn->nrc', back, selector, preferred_element_ty...]
    unnamed x2 -> x0, other arithmetic: 3.16 us -> none
    concatenate x2 -> x3, local copies, waits for them, and re-layouts: 0.99 us -> 3.18 us  [shards(): jnp.concatenate([key_piece.reshape(LIST, row_count, key_width), value_pie...]
  transfers between devices with their start and end apart: 8 -> 3, of which waited for: 7 -> 3; matrix products, arithmetic and copies ran while one was open for 15% -> 8% of each run, Pallas kernels for 0% -> 0%
where the time goes in v1:
time: 89.1 us; the launch traced here: 88.5 us
  waiting for transfers between devices  29.9 us (34%)
  blocking collectives  17.4 us (20%)
  local copies, waits for them, and re-layouts  13.9 us (16%)
  starting transfers between devices  10.8 us (12%)
  matrix products  9.43 us (11%)
  other arithmetic  5.54 us (6%)
  between operations  1.53 us (2%)
    all_to_all x1, blocking collectives, shards(): first_recv = lax.all_to_all(first_send, 'ctx', 0, 0, tiled=True)  17.4 us
    all_to_all x1, waiting for transfers between devices, shards(): lax.all_to_all(pieces.reshape(LIST, peers, chunk_rows, both_width), 'ctx'...  14.2 us
    all_to_all x1, waiting for transfers between devices, shards(): fetched = lax.all_to_all(picked, 'ctx', 0, 2, tiled=True)[0]  11.6 us
    unnamed x16, local copies, waits for them, and re-layouts  5.36 us
    all_to_all x1, waiting for transfers between devices, shards(): lax.all_to_all(summed, 'ctx', 0, 0, tiled=True)  4.13 us
    dot_general x1, matrix products, attend(): jnp.einsum('qgah,jkgh->gaqjk', grad_part, value_part, preferred_element_t...  3.92 us
    all_to_all x1, starting transfers between devices, shards(): lax.all_to_all(pieces.reshape(LIST, peers, chunk_rows, both_width), 'ctx'...  3.64 us
    all_to_all x1, starting transfers between devices, shards(): lax.all_to_all(summed, 'ctx', 0, 0, tiled=True)  3.63 us
  transfers between devices with their start and end apart: 3, of which 3 were waited for; matrix products, arithmetic and copies ran while one was open for 8% of the time, Pallas kernels for 0%

profile of v1, /device:TPU:0, one launch (start us, length us, event | category | flops | bytes accessed | tf_op | source)
XLA Modules:
  0.0 88.5 jit_solution(7649527728791196662)
XLA Ops:
  0.6 0.6 compare_reduce_fusion
  1.9 0.7 convert_bitcast_fusion
  2.6 0.7 broadcast_select_fusion
  3.3 1.0 %maximum_maximum_fusion = bf16[8,16,1152]{2,1,0:T(8,128)(2,1)S(1)} fusion(bf16[8,16,512]{2,1,0:T(8,128)(2,1)} %bitcast.124, bf16[8,16,512]{2,1,0:T(8,128)(2,1)} %bitcast.125, bf16[1152]{0:T(1024)(128)(2,1)S(1)} %fusion.34), kind=kLoop, calls=%fused_computation.33 | loop fusion | flops 884736 | bytes 559360 | tf_op jit(solution)/shard_map/concatenate | solution.py:65
  4.4 17.4 %all_to_all.30 = bf16[8,16,1152]{2,1,0:T(8,128)(2,1)S(1)} all-to-all(bf16[8,16,1152]{2,1,0:T(8,128)(2,1)S(1)} %maximum_maximum_fusion), channel_id=1, replica_groups=mesh['parts'=2,'ctx'=8,'tp'=2] {'ctx'}, dimensions={0} | all-to-all | bytes 589824 | tf_op jit(solution)/shard_map/all_to_all | solution.py:68
  22.1 1.4 %gather_fusion = bf16[16,16,1024]{2,1,0:T(8,128)(2,1)} fusion(bf16[8,16,1024]{2,1,0:T(8,128)(2,1)S(1)} %slice.53, s32[1024]{0:T(1024)S(1)} %pad_clamp_fusion), kind=kCustom, calls=%fused_computation | custom fusion | bytes 1048640 | tf_op jit(solution)/shard_map/jit(_take)/gather | solution.py:74
  23.5 3.5 %all-to-all-start.1 = ((bf16[8,2,16,1024]{3,2,1,0:T(8,128)(2,1)}), bf16[8,2,16,1024]{3,2,1,0:T(8,128)(2,1)S(1)}, u32[]{:S(2)}, u32[]{:S(2)}) async-start(bf16[8,2,16,1024]{3,2,1,0:T(8,128)(2,1)} %bitcast.3), calls=%async_computation.1 | async-start | bytes 1048576 | tf_op jit(solution)/shard_map/all_to_all | solution.py:75
  27.0 0.7 copy.127
  27.7 1.4 %copy.176 = bf16[16,8,32,128]{3,2,1,0:T(8,128)(2,1)S(1)} copy(bf16[16,8,32,128]{3,1,2,0:T(8,128)(2,1)} %bitcast.119) | data formatting | bytes 2097152
  29.1 11.6 %all-to-all-done.1 = bf16[8,2,16,1024]{3,2,1,0:T(8,128)(2,1)S(1)} async-done(((bf16[8,2,16,1024]{3,2,1,0:T(8,128)(2,1)}), bf16[8,2,16,1024]{3,2,1,0:T(8,128)(2,1)S(1)}, u32[]{:S(2)}, u32[]{:S(2)}) %all-to-all-start.1) | async-done | bytes 524320 | tf_op jit(solution)/shard_map/all_to_all | solution.py:75
  40.8 0.8 copy.121
  41.9 1.1 %bitcast_reduce_fusion = (f32[4,8,128]{2,1,0:T(8,128)S(1)}, f32[4,2,128,128,8]{3,2,4,1,0:T(8,128)S(1)}) fusion(pred[2]{0:T(512)(128)(4,1)S(1)} %iota_compare_fusion.3, bf16[128,4,8,128,1]{3,2,1,0,4:T(8,128)(2,1)S(1)} %bitcast.113, bf16[2,128,4,128,1]{1,3,2,0,4:T(8,128)(2,1)S(1)} %bitcast.117), kind=kOutput, calls=%fused_computation.5 | convolution fusion | flops 271577088 | bytes 5521410 | tf_op jit(solution)/shard_map/qgah,jkgh->gaqjk/dot_general | solution.py:15
  42.9 1.0 %fusion.4 = f32[4,8,128]{2,1,0:T(8,128)S(1)} fusion(f32[4,2,128,128,8]{3,2,4,1,0:T(8,128)S(1)} %get-tuple-element.45, f32[4,8,128]{2,1,0:T(8,128)S(1)} %get-tuple-element.44, pred[2]{0:T(512)(128)(4,1)S(1)} %iota_compare_fusion.3), kind=kLoop, calls=%fused_computation.9 | loop fusion | flops 4190208 | bytes 4227074 | tf_op jit(solution)/shard_map/reduce_sum | solution.py:21
  43.9 1.1 %fusion.37 = bf16[4,8,128,2,128]{2,4,1,3,0:T(8,128)(2,1)S(1)} fusion(f32[4,8,128]{2,1,0:T(8,128)S(1)} %fusion.4, f32[4,8,128]{2,1,0:T(8,128)S(1)} %get-tuple-element.44, f32[4,2,128,128,8]{3,2,4,1,0:T(8,128)S(1)} %get-tuple-element.45, pred[2]{0:T(512)(128)(4,1)S(1)} %iota_compare_fusion.3), kind=kLoop, calls=%fused_computation.55 | loop fusion | flops 5242880 | bytes 6324226 | tf_op jit(solution)/shard_map/convert_element_type | solution.py:22
  45.0 0.7 fusion.21
  45.7 0.5 fusion.14
  46.2 0.9 %copy.135 = bf16[2,128,4,128]{3,2,1,0:T(4,128)(2,1)} copy(bf16[2,128,4,128]{3,1,0,2:T(8,128)(2,1)S(1)} %fusion.21) | data formatting | bytes 524288 | tf_op jit(solution)/shard_map/gaqjk,qgah->jkgh/transpose | solution.py:41
  47.1 1.7 %concatenate.31 = bf16[2,8,16,512]{3,2,1,0:T(8,128)(2,1)} reshape(bf16[2,128,4,128]{3,2,1,0:T(4,128)(2,1)} %copy.135) | data formatting | bytes 524288 | tf_op jit(solution)/shard_map/concatenate | solution.py:86
  49.2 3.9 %fusion.1 = bf16[4,8,128,2,128]{2,4,1,3,0:T(8,128)(2,1)S(1)} fusion(bf16[128,4,8,128,1]{0,3,2,4,1:T(8,128)(2,1)S(1)} %bitcast.112, f32[4,8,128]{2,1,0:T(8,128)S(1)} %bitcast.126, bf16[2,128,4,128,1]{1,3,2,0,4:T(8,128)(2,1)} %bitcast.122, f32[4,8,128]{2,1,0:T(8,128)S(1)} %fusion.4, f32[4,8,128]{2,1,0:T(8,128)S(1)} %get-tuple-element.44, ...), kind=kOutput, calls=%fused_computation.3 | convolution fusion | flops 275775488 | bytes 7651330 | tf_op jit(solution)/shard_map/qgah,jkgh->gaqjk/dot_general | solution.py:28
  53.2 0.8 fusion.22
  54.0 0.5 copy-done.4
  54.9 1.3 %copy.136 = bf16[2,8,16,1024]{3,0,2,1:T(2,128)(2,1)} copy(bf16[2,8,16,1024]{3,2,1,0:T(8,128)(2,1)S(1)} %pad_maximum_fusion) | data formatting | bytes 1048576 | tf_op jit(solution)/shard_map/concatenate | solution.py:86
  56.2 3.6 %all-to-all-start.2 = ((bf16[2,8,16,1024]{3,0,2,1:T(2,128)(2,1)}), bf16[2,8,16,1024]{3,0,2,1:T(2,128)(2,1)S(1)}, u32[]{:S(2)}, u32[]{:S(2)}) async-start(bf16[2,8,16,1024]{3,0,2,1:T(2,128)(2,1)} %copy.136), calls=%async_computation.2 | async-start | bytes 1048576 | tf_op jit(solution)/shard_map/all_to_all | solution.py:93
  59.9 14.2 %all-to-all-done.2 = bf16[2,8,16,1024]{3,0,2,1:T(2,128)(2,1)S(1)} async-done(((bf16[2,8,16,1024]{3,0,2,1:T(2,128)(2,1)}), bf16[2,8,16,1024]{3,0,2,1:T(2,128)(2,1)S(1)}, u32[]{:S(2)}, u32[]{:S(2)}) %all-to-all-start.2) | async-done | bytes 524320 | tf_op jit(solution)/shard_map/all_to_all | solution.py:93
  74.0 0.4 fusion.20
  74.4 0.9 copy.138
  75.3 3.6 %all-to-all-start.3 = ((bf16[8,16,1024]{2,1,0:T(8,128)(2,1)}), bf16[8,16,1024]{2,1,0:T(8,128)(2,1)S(1)}, u32[]{:S(2)}, u32[]{:S(2)}) async-start(bf16[8,16,1024]{2,1,0:T(8,128)(2,1)} %copy.138), calls=%async_computation.3 | async-start | bytes 524288 | tf_op jit(solution)/shard_map/all_to_all | solution.py:105
  78.9 2.1 %fusion.5 = bf16[4,128,8,128]{3,1,2,0:T(8,128)(2,1)S(1)} fusion(bf16[4,8,128,2,128]{2,4,1,3,0:T(8,128)(2,1)} %copy-done.4, bf16[2,128,4,128,1]{1,3,2,0,4:T(8,128)(2,1)S(1)} %bitcast.118), kind=kOutput, calls=%fused_computation.11 | convolution fusion | flops 269484032 | bytes 3407872 | tf_op jit(solution)/shard_map/gaqjk,jkgh->qgah/dot_general | solution.py:36
  81.0 1.3 %copy.140 = bf16[128,4096]{1,0:T(8,128)(2,1)} copy(bf16[128,4096]{0,1:T(8,128)(2,1)S(1)} %bitcast.120) | data formatting | bytes 2097152
  82.4 1.3 %copy.139 = bf16[128,4096]{1,0:T(8,128)(2,1)} copy(bf16[128,4096]{0,1:T(8,128)(2,1)S(1)} %bitcast.110) | data formatting | bytes 2097152
  83.7 4.1 %all-to-all-done.3 = bf16[8,16,1024]{2,1,0:T(8,128)(2,1)S(1)} async-done(((bf16[8,16,1024]{2,1,0:T(8,128)(2,1)}), bf16[8,16,1024]{2,1,0:T(8,128)(2,1)S(1)}, u32[]{:S(2)}, u32[]{:S(2)}) %all-to-all-start.3) | async-done | bytes 262176 | tf_op jit(solution)/shard_map/all_to_all | solution.py:105
  87.8 0.7 slice_bitcast_fusion
  (29 shorter events, 1.4 us)
Async XLA Ops:
  0.6 26.4 %copy-start.1 = (bf16[128,4096]{1,0:T(8,128)(2,1)S(1)}, bf16[128,4096]{1,0:T(8,128)(2,1)}, u32[]{:S(2)}) copy-start(bf16[128,4096]{1,0:T(8,128)(2,1)} %param.11) | copy-start | bytes 3145732
  23.5 17.3 %all-to-all-start.1 = ((bf16[8,2,16,1024]{3,2,1,0:T(8,128)(2,1)}), bf16[8,2,16,1024]{3,2,1,0:T(8,128)(2,1)S(1)}, u32[]{:S(2)}, u32[]{:S(2)}) async-start(bf16[8,2,16,1024]{3,2,1,0:T(8,128)(2,1)} %bitcast.3), calls=%async_computation.1 | async-start | bytes 1048576 | tf_op jit(solution)/shard_map/all_to_all | solution.py:75
  42.9 2.1 %copy-start = (f32[4,2,128,128,8]{3,2,4,1,0:T(8,128)}, f32[4,2,128,128,8]{3,2,4,1,0:T(8,128)S(1)}, u32[]{:S(2)}) copy-start(f32[4,2,128,128,8]{3,2,4,1,0:T(8,128)S(1)} %get-tuple-element.45) | copy-start | bytes 12582916
  43.9 1.8 %copy-start.3 = (bf16[2,128,512]{1,2,0:T(8,128)(2,1)S(1)}, bf16[2,128,512]{1,2,0:T(8,128)(2,1)}, u32[]{:S(2)}) copy-start(bf16[2,128,512]{1,2,0:T(8,128)(2,1)} %copy.121) | copy-start | bytes 786436
  53.1 1.3 %copy-start.4 = (bf16[4,8,128,2,128]{2,4,1,3,0:T(8,128)(2,1)}, bf16[4,8,128,2,128]{2,4,1,3,0:T(8,128)(2,1)S(1)}, u32[]{:S(2)}) copy-start(bf16[4,8,128,2,128]{2,4,1,3,0:T(8,128)(2,1)S(1)} %fusion.1) | copy-start | bytes 6291460
  53.1 1.6 %copy-start.2 = (bf16[2,8,16,512]{3,2,1,0:T(8,128)(2,1)S(1)}, bf16[2,8,16,512]{3,2,1,0:T(8,128)(2,1)}, u32[]{:S(2)}) copy-start(bf16[2,8,16,512]{3,2,1,0:T(8,128)(2,1)} %concatenate.31) | copy-start | bytes 786436
  56.2 17.8 %all-to-all-start.2 = ((bf16[2,8,16,1024]{3,0,2,1:T(2,128)(2,1)}), bf16[2,8,16,1024]{3,0,2,1:T(2,128)(2,1)S(1)}, u32[]{:S(2)}, u32[]{:S(2)}) async-start(bf16[2,8,16,1024]{3,0,2,1:T(2,128)(2,1)} %copy.136), calls=%async_computation.2 | async-start | bytes 1048576 | tf_op jit(solution)/shard_map/all_to_all | solution.py:93
  75.3 12.5 %all-to-all-start.3 = ((bf16[8,16,1024]{2,1,0:T(8,128)(2,1)}), bf16[8,16,1024]{2,1,0:T(8,128)(2,1)S(1)}, u32[]{:S(2)}, u32[]{:S(2)}) async-start(bf16[8,16,1024]{2,1,0:T(8,128)(2,1)} %copy.138), calls=%async_computation.3 | async-start | bytes 524288 | tf_op jit(solution)/shard_map/all_to_all | solution.py:105

commit v2 on v1

v2 whole, which is shorter than its diff:
```python
import jax
import jax.numpy as jnp
from jax import lax
from jax.experimental import pallas as pl
from jax.experimental.pallas import tpu as pltpu
from jax.sharding import PartitionSpec as P

QUERY_HEADS = 64
KEY_VALUE_HEADS = 8
HEAD_SIZE = 128
LIST = 2
TAG_COLUMNS = 128


def attention_kernel(chunk_rows, heads_per_group):
    score_scale = HEAD_SIZE ** (-0.5)

    def kernel(count_ref, q_ref, do_ref, k_ref, v_ref, o_ref, dq_ref, dk_ref, dv_ref):
        keys = k_ref[...]
        values = v_ref[...]
        key_total = keys.shape[0]
        slot = (lax.broadcasted_iota(jnp.int32, (1, key_total), 1) // chunk_rows) % LIST
        live = slot < count_ref[0]
        nt = (((1,), (1,)), ((), ()))
        tn = (((0,), (0,)), ((), ()))
        key_acc = jnp.zeros((key_total, HEAD_SIZE), jnp.float32)
        value_acc = jnp.zeros((key_total, HEAD_SIZE), jnp.float32)
        for head in range(heads_per_group):
            cols = slice(head * HEAD_SIZE, (head + 1) * HEAD_SIZE)
            q = q_ref[:, cols]
            do = do_ref[:, cols]
            scores = score_scale * lax.dot_general(
                q, keys, nt, preferred_element_type=jnp.float32
            )
            masked = jnp.where(live, scores, -jnp.inf)
            peak = jnp.max(masked, axis=1, keepdims=True)
            exponent = jnp.exp(masked - peak)
            weights = exponent / jnp.sum(exponent, axis=1, keepdims=True)
            weights_low = weights.astype(jnp.bfloat16)
            attended = jnp.dot(
                weights_low, values, preferred_element_type=jnp.float32
            ).astype(jnp.bfloat16)
            o_ref[:, cols] = attended
            row_delta = jnp.sum(
                do.astype(jnp.float32) * attended.astype(jnp.float32), axis=1, keepdims=True
            )
            weight_grad = lax.dot_general(do, values, nt, preferred_element_type=jnp.float32)
            score_grad = (weights * (weight_grad - row_delta)).astype(jnp.bfloat16)
            dq_ref[:, cols] = (
                score_scale * jnp.dot(score_grad, keys, preferred_element_type=jnp.float32)
            ).astype(jnp.bfloat16)
            key_acc = key_acc + lax.dot_general(
                score_grad, q, tn, preferred_element_type=jnp.float32
            )
            value_acc = value_acc + lax.dot_general(
                weights_low, do, tn, preferred_element_type=jnp.float32
            )
        dk_ref[...] = (score_scale * key_acc).astype(jnp.bfloat16)
        dv_ref[...] = value_acc.astype(jnp.bfloat16)

    return kernel


def attend_all(queries, output_gradient, fetched, count, chunk_rows):
    query_rows, query_width = queries.shape
    key_total, both_width = fetched.shape
    key_width = both_width // 2
    local_groups = key_width // HEAD_SIZE
    heads_per_group = QUERY_HEADS // KEY_VALUE_HEADS
    group_width = heads_per_group * HEAD_SIZE
    row_block = pl.BlockSpec((query_rows, group_width), lambda g: (0, g))
    key_block = pl.BlockSpec((key_total, HEAD_SIZE), lambda g: (0, g))
    value_block = pl.BlockSpec((key_total, HEAD_SIZE), lambda g: (0, local_groups + g))
    return pl.pallas_call(
        attention_kernel(chunk_rows, heads_per_group),
        grid=(local_groups,),
        in_specs=[
            pl.BlockSpec(memory_space=pltpu.SMEM),
            row_block,
            row_block,
            key_block,
            value_block,
        ],
        out_specs=[row_block, row_block, key_block, key_block],
        out_shape=[
            jax.ShapeDtypeStruct((query_rows, query_width), jnp.bfloat16),
            jax.ShapeDtypeStruct((query_rows, query_width), jnp.bfloat16),
            jax.ShapeDtypeStruct((key_total, key_width), jnp.bfloat16),
            jax.ShapeDtypeStruct((key_total, key_width), jnp.bfloat16),
        ],
    )(count, queries, output_gradient, fetched, fetched)


def make_shards(peers):
    def shards(
        queries, episode_key_cache, episode_value_cache, output_gradient, block_lists, block_counts
    ):
        row_count = episode_key_cache.shape[0]
        key_width = episode_key_cache.shape[2]
        both_width = 2 * key_width
        chunk_rows = row_count // peers

        held = jnp.concatenate(
            [episode_key_cache[:, 0, :], episode_value_cache[:, 0, :]], axis=1
        )
        tag = jnp.concatenate([block_lists[0], block_counts]).astype(jnp.bfloat16)
        tag_block = jnp.zeros((row_count, TAG_COLUMNS), jnp.bfloat16)
        tag_block = tag_block.at[:, : LIST + 1].set(jnp.broadcast_to(tag, (row_count, LIST + 1)))
        first_send = jnp.concatenate([held, tag_block], axis=1).reshape(
            peers, chunk_rows, both_width + TAG_COLUMNS
        )
        first_recv = lax.all_to_all(first_send, "ctx", 0, 0, tiled=True)
        info = first_recv[:, 0, both_width : both_width + LIST + 1].astype(jnp.int32)
        lists_all = info[:, :LIST]
        counts_all = info[:, LIST]

        rows_held = first_recv[:, :, :both_width]
        picked = jnp.take(rows_held, lists_all, axis=0, mode="clip")
        fetched = lax.all_to_all(picked, "ctx", 0, 0, tiled=True).reshape(
            LIST * row_count, both_width
        )
        attn_out, query_grad, key_piece, value_piece = attend_all(
            queries,
            output_gradient,
            fetched,
            block_counts,
            chunk_rows,
        )

        pieces = jnp.concatenate([key_piece, value_piece], axis=1).reshape(
            peers, LIST, chunk_rows, both_width
        )
        back = lax.all_to_all(pieces, "ctx", 0, 0, tiled=True)
        slot_live = jnp.arange(LIST, dtype=jnp.int32)[None, :] < counts_all[:, None]
        selector = (
            (lists_all[:, :, None] == jnp.arange(peers, dtype=jnp.int32)[None, None, :])
            & slot_live[:, :, None]
        ).astype(jnp.bfloat16)
        summed = jnp.einsum(
            "qjrc,qjn->nrc", back, selector, preferred_element_type=jnp.float32
        ).astype(jnp.bfloat16)

        owned = lax.all_to_all(summed, "ctx", 0, 0, tiled=True).reshape(row_count, both_width)
        key_cache_gradient = owned[:, None, :key_width]
        value_cache_gradient = owned[:, None, key_width:]
        return attn_out, query_grad, key_cache_gradient, value_cache_gradient

    return shards


def solution(mesh):
    placed = (
        P(("parts", "ctx"), "tp"),
        P(None, ("parts", "ctx"), "tp"),
        P(None, ("parts", "ctx"), "tp"),
        P(("parts", "ctx"), "tp"),
        P(("parts", "ctx"), None),
        P(("parts", "ctx")),
    )
    return jax.shard_map(
        make_shards(mesh.shape["ctx"]),
        mesh=mesh,
        in_specs=placed,
        out_specs=(
            P(("parts", "ctx"), "tp"),
            P(("parts", "ctx"), "tp"),
            P(None, ("parts", "ctx"), "tp"),
            P(None, ("parts", "ctx"), "tp"),
        ),
        check_vma=False,
    )
```

time: 89.1 us -> 95.7 us (1.074)
  blocking collectives: 17.4 us -> 46.8 us
  Pallas kernels: 0 us -> 21.8 us
  waiting for transfers between devices: 29.9 us -> 14.1 us
  local copies, waits for them, and re-layouts: 13.9 us -> 3.74 us
  matrix products: 9.43 us -> 0.39 us
  starting transfers between devices: 10.8 us -> 3.63 us
  other arithmetic: 5.54 us -> 3.49 us
    all_to_all x0 -> x2, blocking collectives: none -> 29.4 us  [the longest x1 17.1 us: shards(): lax.all_to_all(picked, 'ctx', 0, 0, tiled=True)]
    pallas_call x0 -> x1, Pallas kernels: none -> 21.8 us  [attend_all(): pl.pallas_call(attention_kernel(chunk_rows, heads_per_group), grid=(local...]
    all_to_all x3 -> x1, waiting for transfers between devices: 29.9 us -> 14.1 us  [shards(): back = lax.all_to_all(pieces, 'ctx', 0, 0, tiled=True)]
    dot_general x7 -> x1, matrix products: 9.43 us -> 0.39 us  [shards(): jnp.einsum('qjrc,qjn->nrc', back, selector, preferred_element_type=jnp.fl...]
    all_to_all x3 -> x1, starting transfers between devices: 10.8 us -> 3.63 us  [shards(): back = lax.all_to_all(pieces, 'ctx', 0, 0, tiled=True)]
    unnamed x16 -> x4, local copies, waits for them, and re-layouts: 5.36 us -> 0.75 us
    concatenate x3 -> x0, local copies, waits for them, and re-layouts: 3.18 us -> none  [shards(): jnp.concatenate([key_piece.reshape(LIST, row_count, key_width), value_pie...]
    reduce_sum x2 -> x0, other arithmetic: 1.34 us -> none  [the longest x1 0.96 us: attend(): weights = exponent / jnp.sum(exponent, axis=(3, 4), keepdims=True)]
  transfers between devices with their start and end apart: 3 -> 1, of which waited for: 3 -> 1; matrix products, arithmetic and copies ran while one was open for 8% -> 0% of each run, Pallas kernels for 0% -> 0%
where the time goes in v2:
time: 95.7 us; the launch traced here: 95.3 us
  blocking collectives  46.8 us (49%)
  Pallas kernels  21.8 us (23%)
  waiting for transfers between devices  14.1 us (15%)
  local copies, waits for them, and re-layouts  3.74 us (4%)
  starting transfers between devices  3.63 us (4%)
  other arithmetic  3.49 us (4%)
  between operations  1.36 us (1%)
    pallas_call x1, Pallas kernels, attend_all(): pl.pallas_call(attention_kernel(chunk_rows, heads_per_group), grid=(local...  21.8 us
    all_to_all x1, blocking collectives, shards(): first_recv = lax.all_to_all(first_send, 'ctx', 0, 0, tiled=True)  17.4 us
    all_to_all x1, blocking collectives, shards(): lax.all_to_all(picked, 'ctx', 0, 0, tiled=True)  17.1 us
    all_to_all x1, waiting for transfers between devices, shards(): back = lax.all_to_all(pieces, 'ctx', 0, 0, tiled=True)  14.1 us
    all_to_all x1, blocking collectives, shards(): lax.all_to_all(summed, 'ctx', 0, 0, tiled=True)  12.3 us
    all_to_all x1, starting transfers between devices, shards(): back = lax.all_to_all(pieces, 'ctx', 0, 0, tiled=True)  3.63 us
  transfers between devices with their start and end apart: 1, of which 1 were waited for; matrix products, arithmetic and copies ran while one was open for 0% of the time, Pallas kernels for 0%

profile of v2, /device:TPU:0, one launch (start us, length us, event | category | flops | bytes accessed | tf_op | source)
XLA Modules:
  0.0 95.3 jit_solution(8860312756781914518)
XLA Ops:
  0.6 0.6 compare_reduce_fusion
  1.9 0.0 copy-start
  1.9 0.6 copy-done
  2.6 0.7 broadcast_select_fusion
  3.3 1.0 %maximum_maximum_fusion = bf16[8,16,1152]{2,1,0:T(8,128)(2,1)S(1)} fusion(bf16[8,16,512]{2,1,0:T(8,128)(2,1)} %bitcast.30, bf16[8,16,512]{2,1,0:T(8,128)(2,1)} %bitcast.31, bf16[1152]{0:T(1024)(128)(2,1)S(1)} %fusion.5), kind=kLoop, calls=%fused_computation.5 | loop fusion | flops 884736 | bytes 559360 | tf_op jit(solution)/shard_map/concatenate | solution.py:109
  4.3 17.4 %all_to_all.20 = bf16[8,16,1152]{2,1,0:T(8,128)(2,1)S(1)} all-to-all(bf16[8,16,1152]{2,1,0:T(8,128)(2,1)S(1)} %maximum_maximum_fusion), channel_id=1, replica_groups=mesh['parts'=2,'ctx'=8,'tp'=2] {'ctx'}, dimensions={0} | all-to-all | bytes 589824 | tf_op jit(solution)/shard_map/all_to_all | solution.py:112
  21.8 0.1 copy.43
  21.9 0.1 copy.37
  22.0 0.1 reshape.78
  22.1 0.6 gather_fusion
  22.7 17.1 %all_to_all.21 = bf16[8,2,16,1024]{3,2,1,0:T(8,128)(2,1)} all-to-all(bf16[8,2,16,1024]{3,2,1,0:T(8,128)(2,1)S(1)} %bitcast.27), channel_id=1, replica_groups=mesh['parts'=2,'ctx'=8,'tp'=2] {'ctx'}, dimensions={0} | all-to-all | bytes 1048576 | tf_op jit(solution)/shard_map/all_to_all | solution.py:119
  39.8 21.8 %shard_map.93 = (bf16[128,4096]{1,0:T(8,128)(2,1)}, bf16[128,4096]{1,0:T(8,128)(2,1)}, bf16[256,512]{1,0:T(8,128)(2,1)}, bf16[256,512]{1,0:T(8,128)(2,1)}) custom-call(s32[1]{0:T(128)S(6)} %copy.48.count_ref, bf16[128,4096]{1,0:T(8,128)(2,1)} %q_ref.1, bf16[128,4096]{1,0:T(8,128)(2,1)} %do_ref.1, bf16[256,1024]{1,0:T(8,128)(2,1)} %bitcast.25, ...), custom_call_target="tpu_custom_call" | custom-call | tf_op jit(solution)/shard_map/pallas_call | solution.py:74
  61.6 1.1 %pad_maximum_fusion = bf16[256,1024]{1,0:T(8,128)(2,1)S(1)} fusion(bf16[256,512]{1,0:T(8,128)(2,1)} %get-tuple-element.23, bf16[256,512]{1,0:T(8,128)(2,1)} %get-tuple-element.22), kind=kLoop, calls=%fused_computation.3 | loop fusion | flops 1048576 | bytes 1048576 | tf_op jit(solution)/shard_map/concatenate | solution.py:130
  62.7 1.3 %copy.38 = bf16[8,2,16,1024]{3,1,2,0:T(2,128)(2,1)} copy(bf16[8,2,16,1024]{3,2,1,0:T(8,128)(2,1)S(1)} %bitcast.28) | data formatting | bytes 1048576 | tf_op jit(solution)/shard_map/reshape | solution.py:130
  64.1 3.6 %all-to-all-start.2 = ((bf16[8,2,16,1024]{3,1,2,0:T(2,128)(2,1)}), bf16[8,2,16,1024]{3,1,2,0:T(2,128)(2,1)S(1)}, u32[]{:S(2)}, u32[]{:S(2)}) async-start(bf16[8,2,16,1024]{3,1,2,0:T(2,128)(2,1)} %copy.38), calls=%async_computation.2 | async-start | bytes 1048576 | tf_op jit(solution)/shard_map/all_to_all | solution.py:133
  67.7 14.1 %all-to-all-done.2 = bf16[8,2,16,1024]{3,1,2,0:T(2,128)(2,1)S(1)} async-done(((bf16[8,2,16,1024]{3,1,2,0:T(2,128)(2,1)}), bf16[8,2,16,1024]{3,1,2,0:T(2,128)(2,1)S(1)}, u32[]{:S(2)}, u32[]{:S(2)}) %all-to-all-start.2) | async-done | bytes 524320 | tf_op jit(solution)/shard_map/all_to_all | solution.py:133
  81.8 0.4 fusion
  82.2 0.2 copy.40
  82.4 12.3 %all_to_all.22 = bf16[8,16,1024]{2,1,0:T(8,128)(2,1)S(1)} all-to-all(bf16[8,16,1024]{2,1,0:T(8,128)(2,1)S(1)} %copy.40), channel_id=1, replica_groups=mesh['parts'=2,'ctx'=8,'tp'=2] {'ctx'}, dimensions={0} | all-to-all | bytes 524288 | tf_op jit(solution)/shard_map/all_to_all | solution.py:143
  94.6 0.7 slice_bitcast_fusion
  (10 shorter events, 0.1 us)
Async XLA Ops:
  1.9 0.7 copy-start
  64.1 17.7 %all-to-all-start.2 = ((bf16[8,2,16,1024]{3,1,2,0:T(2,128)(2,1)}), bf16[8,2,16,1024]{3,1,2,0:T(2,128)(2,1)S(1)}, u32[]{:S(2)}, u32[]{:S(2)}) async-start(bf16[8,2,16,1024]{3,1,2,0:T(2,128)(2,1)} %copy.38), calls=%async_computation.2 | async-start | bytes 1048576 | tf_op jit(solution)/shard_map/all_to_all | solution.py:133

commit v3 on v2

--- a/solution.py
+++ b/solution.py
@@ -19,44 +19,40 @@
         keys = k_ref[...]
         values = v_ref[...]
         key_total = keys.shape[0]
+        query_rows = q_ref.shape[0]
         slot = (lax.broadcasted_iota(jnp.int32, (1, key_total), 1) // chunk_rows) % LIST
         live = slot < count_ref[0]
         nt = (((1,), (1,)), ((), ()))
         tn = (((0,), (0,)), ((), ()))
-        key_acc = jnp.zeros((key_total, HEAD_SIZE), jnp.float32)
-        value_acc = jnp.zeros((key_total, HEAD_SIZE), jnp.float32)
-        for head in range(heads_per_group):
-            cols = slice(head * HEAD_SIZE, (head + 1) * HEAD_SIZE)
-            q = q_ref[:, cols]
-            do = do_ref[:, cols]
-            scores = score_scale * lax.dot_general(
-                q, keys, nt, preferred_element_type=jnp.float32
-            )
-            masked = jnp.where(live, scores, -jnp.inf)
-            peak = jnp.max(masked, axis=1, keepdims=True)
-            exponent = jnp.exp(masked - peak)
-            weights = exponent / jnp.sum(exponent, axis=1, keepdims=True)
-            weights_low = weights.astype(jnp.bfloat16)
-            attended = jnp.dot(
-                weights_low, values, preferred_element_type=jnp.float32
-            ).astype(jnp.bfloat16)
-            o_ref[:, cols] = attended
-            row_delta = jnp.sum(
-                do.astype(jnp.float32) * attended.astype(jnp.float32), axis=1, keepdims=True
-            )
-            weight_grad = lax.dot_general(do, values, nt, preferred_element_type=jnp.float32)
-            score_grad = (weights * (weight_grad - row_delta)).astype(jnp.bfloat16)
-            dq_ref[:, cols] = (
-                score_scale * jnp.dot(score_grad, keys, preferred_element_type=jnp.float32)
-            ).astype(jnp.bfloat16)
-            key_acc = key_acc + lax.dot_general(
-                score_grad, q, tn, preferred_element_type=jnp.float32
-            )
-            value_acc = value_acc + lax.dot_general(
-                weights_low, do, tn, preferred_element_type=jnp.float32
-            )
-        dk_ref[...] = (score_scale * key_acc).astype(jnp.bfloat16)
-        dv_ref[...] = value_acc.astype(jnp.bfloat16)
+        heads = [slice(a * HEAD_SIZE, (a + 1) * HEAD_SIZE) for a in range(heads_per_group)]
+        q = jnp.concatenate([q_ref[:, cols] for cols in heads], axis=0)
+        do = jnp.concatenate([do_ref[:, cols] for cols in heads], axis=0)
+        scores = score_scale * lax.dot_general(q, keys, nt, preferred_element_type=jnp.float32)
+        masked = jnp.where(live, scores, -jnp.inf)
+        peak = jnp.max(masked, axis=1, keepdims=True)
+        exponent = jnp.exp(masked - peak)
+        weights = exponent / jnp.sum(exponent, axis=1, keepdims=True)
+        weights_low = weights.astype(jnp.bfloat16)
+        attended = jnp.dot(weights_low, values, preferred_element_type=jnp.float32).astype(
+            jnp.bfloat16
+        )
+        row_delta = jnp.sum(
+            do.astype(jnp.float32) * attended.astype(jnp.float32), axis=1, keepdims=True
+        )
+        weight_grad = lax.dot_general(do, values, nt, preferred_element_type=jnp.float32)
+        score_grad = (weights * (weight_grad - row_delta)).astype(jnp.bfloat16)
+        query_grad = (
+            score_scale * jnp.dot(score_grad, keys, preferred_element_type=jnp.float32)
+        ).astype(jnp.bfloat16)
+        for a, cols in enumerate(heads):
+            o_ref[:, cols] = attended[a * query_rows : (a + 1) * query_rows]
+            dq_ref[:, cols] = query_grad[a * query_rows : (a + 1) * query_rows]
+        dk_ref[...] = (
+            score_scale * lax.dot_general(score_grad, q, tn, preferred_element_type=jnp.float32)
+        ).astype(jnp.bfloat16)
+        dv_ref[...] = lax.dot_general(
+            weights_low, do, tn, preferred_element_type=jnp.float32
+        ).astype(jnp.bfloat16)
 
     return kernel
 

time: 95.7 us -> 81.6 us (0.85)
  Pallas kernels: 21.8 us -> 7.71 us
    pallas_call x1, Pallas kernels: 21.8 us -> 7.71 us  [attend_all(): pl.pallas_call(attention_kernel(chunk_rows, heads_per_group), grid=(local...]
where the time goes in v3:
time: 81.6 us; the launch traced here: 81.2 us
  blocking collectives  46.8 us (57%)
  waiting for transfers between devices  14.1 us (17%)
  Pallas kernels  7.71 us (9%)
  local copies, waits for them, and re-layouts  3.74 us (5%)
  starting transfers between devices  3.64 us (4%)
  other arithmetic  3.49 us (4%)
  between operations  1.36 us (2%)
    all_to_all x1, blocking collectives, shards(): first_recv = lax.all_to_all(first_send, 'ctx', 0, 0, tiled=True)  17.4 us
    all_to_all x1, blocking collectives, shards(): lax.all_to_all(picked, 'ctx', 0, 0, tiled=True)  17.1 us
    all_to_all x1, waiting for transfers between devices, shards(): back = lax.all_to_all(pieces, 'ctx', 0, 0, tiled=True)  14.1 us
    all_to_all x1, blocking collectives, shards(): lax.all_to_all(summed, 'ctx', 0, 0, tiled=True)  12.3 us
    pallas_call x1, Pallas kernels, attend_all(): pl.pallas_call(attention_kernel(chunk_rows, heads_per_group), grid=(local...  7.71 us
    all_to_all x1, starting transfers between devices, shards(): back = lax.all_to_all(pieces, 'ctx', 0, 0, tiled=True)  3.64 us
  transfers between devices with their start and end apart: 1, of which 1 were waited for; matrix products, arithmetic and copies ran while one was open for 0% of the time, Pallas kernels for 0%

profile of v3, /device:TPU:0, one launch (start us, length us, event | category | flops | bytes accessed | tf_op | source)
XLA Modules:
  0.0 81.2 jit_solution(16687882825640351829)
XLA Ops:
  0.6 0.6 compare_reduce_fusion
  1.9 0.0 copy-start
  1.9 0.6 copy-done
  2.6 0.7 broadcast_select_fusion
  3.3 1.0 %maximum_maximum_fusion = bf16[8,16,1152]{2,1,0:T(8,128)(2,1)S(1)} fusion(bf16[8,16,512]{2,1,0:T(8,128)(2,1)} %bitcast.30, bf16[8,16,512]{2,1,0:T(8,128)(2,1)} %bitcast.31, bf16[1152]{0:T(1024)(128)(2,1)S(1)} %fusion.5), kind=kLoop, calls=%fused_computation.5 | loop fusion | flops 884736 | bytes 559360 | tf_op jit(solution)/shard_map/concatenate | solution.py:105
  4.3 17.4 %all_to_all.20 = bf16[8,16,1152]{2,1,0:T(8,128)(2,1)S(1)} all-to-all(bf16[8,16,1152]{2,1,0:T(8,128)(2,1)S(1)} %maximum_maximum_fusion), channel_id=1, replica_groups=mesh['parts'=2,'ctx'=8,'tp'=2] {'ctx'}, dimensions={0} | all-to-all | bytes 589824 | tf_op jit(solution)/shard_map/all_to_all | solution.py:108
  21.8 0.1 copy.43
  21.9 0.1 copy.37
  22.0 0.1 reshape.78
  22.1 0.6 gather_fusion
  22.7 17.1 %all_to_all.21 = bf16[8,2,16,1024]{3,2,1,0:T(8,128)(2,1)} all-to-all(bf16[8,2,16,1024]{3,2,1,0:T(8,128)(2,1)S(1)} %bitcast.27), channel_id=1, replica_groups=mesh['parts'=2,'ctx'=8,'tp'=2] {'ctx'}, dimensions={0} | all-to-all | bytes 1048576 | tf_op jit(solution)/shard_map/all_to_all | solution.py:115
  39.8 7.7 %shard_map.93 = (bf16[128,4096]{1,0:T(8,128)(2,1)}, bf16[128,4096]{1,0:T(8,128)(2,1)}, bf16[256,512]{1,0:T(8,128)(2,1)}, bf16[256,512]{1,0:T(8,128)(2,1)}) custom-call(s32[1]{0:T(128)S(6)} %copy.48.count_ref, bf16[128,4096]{1,0:T(8,128)(2,1)} %q_ref.1, bf16[128,4096]{1,0:T(8,128)(2,1)} %do_ref.1, bf16[256,1024]{1,0:T(8,128)(2,1)} %bitcast.25, ...), custom_call_target="tpu_custom_call" | custom-call | tf_op jit(solution)/shard_map/pallas_call | solution.py:70
  47.5 1.1 %pad_maximum_fusion = bf16[256,1024]{1,0:T(8,128)(2,1)S(1)} fusion(bf16[256,512]{1,0:T(8,128)(2,1)} %get-tuple-element.23, bf16[256,512]{1,0:T(8,128)(2,1)} %get-tuple-element.22), kind=kLoop, calls=%fused_computation.3 | loop fusion | flops 1048576 | bytes 1048576 | tf_op jit(solution)/shard_map/concatenate | solution.py:126
  48.6 1.3 %copy.38 = bf16[8,2,16,1024]{3,1,2,0:T(2,128)(2,1)} copy(bf16[8,2,16,1024]{3,2,1,0:T(8,128)(2,1)S(1)} %bitcast.28) | data formatting | bytes 1048576 | tf_op jit(solution)/shard_map/reshape | solution.py:126
  49.9 3.6 %all-to-all-start.2 = ((bf16[8,2,16,1024]{3,1,2,0:T(2,128)(2,1)}), bf16[8,2,16,1024]{3,1,2,0:T(2,128)(2,1)S(1)}, u32[]{:S(2)}, u32[]{:S(2)}) async-start(bf16[8,2,16,1024]{3,1,2,0:T(2,128)(2,1)} %copy.38), calls=%async_computation.2 | async-start | bytes 1048576 | tf_op jit(solution)/shard_map/all_to_all | solution.py:129
  53.6 14.1 %all-to-all-done.2 = bf16[8,2,16,1024]{3,1,2,0:T(2,128)(2,1)S(1)} async-done(((bf16[8,2,16,1024]{3,1,2,0:T(2,128)(2,1)}), bf16[8,2,16,1024]{3,1,2,0:T(2,128)(2,1)S(1)}, u32[]{:S(2)}, u32[]{:S(2)}) %all-to-all-start.2) | async-done | bytes 524320 | tf_op jit(solution)/shard_map/all_to_all | solution.py:129
  67.7 0.4 fusion
  68.1 0.2 copy.40
  68.2 12.3 %all_to_all.22 = bf16[8,16,1024]{2,1,0:T(8,128)(2,1)S(1)} all-to-all(bf16[8,16,1024]{2,1,0:T(8,128)(2,1)S(1)} %copy.40), channel_id=1, replica_groups=mesh['parts'=2,'ctx'=8,'tp'=2] {'ctx'}, dimensions={0} | all-to-all | bytes 524288 | tf_op jit(solution)/shard_map/all_to_all | solution.py:139
  80.5 0.7 slice_bitcast_fusion
  (10 shorter events, 0.1 us)
Async XLA Ops:
  1.9 0.7 copy-start
  49.9 17.7 %all-to-all-start.2 = ((bf16[8,2,16,1024]{3,1,2,0:T(2,128)(2,1)}), bf16[8,2,16,1024]{3,1,2,0:T(2,128)(2,1)S(1)}, u32[]{:S(2)}, u32[]{:S(2)}) async-start(bf16[8,2,16,1024]{3,1,2,0:T(2,128)(2,1)} %copy.38), calls=%async_computation.2 | async-start | bytes 1048576 | tf_op jit(solution)/shard_map/all_to_all | solution.py:129

commit v4 on v3

--- a/solution.py
+++ b/solution.py
@@ -12,10 +12,10 @@
 TAG_COLUMNS = 128
 
 
-def attention_kernel(chunk_rows, heads_per_group):
+def attention_kernel(chunk_rows, heads_per_group, local_groups):
     score_scale = HEAD_SIZE ** (-0.5)
 
-    def kernel(count_ref, q_ref, do_ref, k_ref, v_ref, o_ref, dq_ref, dk_ref, dv_ref):
+    def kernel(count_ref, q_ref, do_ref, k_ref, v_ref, o_ref, dq_ref, pieces_ref):
         keys = k_ref[...]
         values = v_ref[...]
         key_total = keys.shape[0]
@@ -47,12 +47,21 @@
         for a, cols in enumerate(heads):
             o_ref[:, cols] = attended[a * query_rows : (a + 1) * query_rows]
             dq_ref[:, cols] = query_grad[a * query_rows : (a + 1) * query_rows]
-        dk_ref[...] = (
+        key_piece = (
             score_scale * lax.dot_general(score_grad, q, tn, preferred_element_type=jnp.float32)
         ).astype(jnp.bfloat16)
-        dv_ref[...] = lax.dot_general(
+        value_piece = lax.dot_general(
             weights_low, do, tn, preferred_element_type=jnp.float32
         ).astype(jnp.bfloat16)
+        group = pl.program_id(0)
+        for index in range(local_groups):
+
+            @pl.when(group == index)
+            def _():
+                key_cols = slice(index * HEAD_SIZE, (index + 1) * HEAD_SIZE)
+                value_cols = slice((local_groups + index) * HEAD_SIZE, (local_groups + index + 1) * HEAD_SIZE)
+                pieces_ref[:, key_cols] = key_piece
+                pieces_ref[:, value_cols] = value_piece
 
     return kernel
 
@@ -68,7 +77,7 @@
     key_block = pl.BlockSpec((key_total, HEAD_SIZE), lambda g: (0, g))
     value_block = pl.BlockSpec((key_total, HEAD_SIZE), lambda g: (0, local_groups + g))
     return pl.pallas_call(
-        attention_kernel(chunk_rows, heads_per_group),
+        attention_kernel(chunk_rows, heads_per_group, local_groups),
         grid=(local_groups,),
         in_specs=[
             pl.BlockSpec(memory_space=pltpu.SMEM),
@@ -77,12 +86,11 @@
             key_block,
             value_block,
         ],
-        out_specs=[row_block, row_block, key_block, key_block],
+        out_specs=[row_block, row_block, pl.BlockSpec((key_total, both_width), lambda g: (0, 0))],
         out_shape=[
             jax.ShapeDtypeStruct((query_rows, query_width), jnp.bfloat16),
             jax.ShapeDtypeStruct((query_rows, query_width), jnp.bfloat16),
-            jax.ShapeDtypeStruct((key_total, key_width), jnp.bfloat16),
-            jax.ShapeDtypeStruct((key_total, key_width), jnp.bfloat16),
+            jax.ShapeDtypeStruct((key_total, both_width), jnp.bfloat16),
         ],
     )(count, queries, output_gradient, fetched, fetched)
 
@@ -100,8 +108,9 @@
             [episode_key_cache[:, 0, :], episode_value_cache[:, 0, :]], axis=1
         )
         tag = jnp.concatenate([block_lists[0], block_counts]).astype(jnp.bfloat16)
-        tag_block = jnp.zeros((row_count, TAG_COLUMNS), jnp.bfloat16)
-        tag_block = tag_block.at[:, : LIST + 1].set(jnp.broadcast_to(tag, (row_count, LIST + 1)))
+        tag_block = jnp.broadcast_to(
+            jnp.pad(tag, (0, TAG_COLUMNS - LIST - 1)), (row_count, TAG_COLUMNS)
+        )
         first_send = jnp.concatenate([held, tag_block], axis=1).reshape(
             peers, chunk_rows, both_width + TAG_COLUMNS
         )
@@ -111,11 +120,13 @@
         counts_all = info[:, LIST]
 
         rows_held = first_recv[:, :, :both_width]
-        picked = jnp.take(rows_held, lists_all, axis=0, mode="clip")
+        picked = jnp.take(rows_held, lists_all, axis=0, mode="clip").reshape(
+            peers, LIST * chunk_rows, both_width
+        )
         fetched = lax.all_to_all(picked, "ctx", 0, 0, tiled=True).reshape(
             LIST * row_count, both_width
         )
-        attn_out, query_grad, key_piece, value_piece = attend_all(
+        attn_out, query_grad, pieces = attend_all(
             queries,
             output_gradient,
             fetched,
@@ -123,10 +134,9 @@
             chunk_rows,
         )
 
-        pieces = jnp.concatenate([key_piece, value_piece], axis=1).reshape(
-            peers, LIST, chunk_rows, both_width
-        )
-        back = lax.all_to_all(pieces, "ctx", 0, 0, tiled=True)
+        back = lax.all_to_all(
+            pieces.reshape(peers, LIST * chunk_rows, both_width), "ctx", 0, 0, tiled=True
+        ).reshape(peers, LIST, chunk_rows, both_width)
         slot_live = jnp.arange(LIST, dtype=jnp.int32)[None, :] < counts_all[:, None]
         selector = (
             (lists_all[:, :, None] == jnp.arange(peers, dtype=jnp.int32)[None, None, :])

time: 81.6 us -> 78.4 us (0.961)
  other arithmetic: 3.49 us -> 1.13 us
  local copies, waits for them, and re-layouts: 3.74 us -> 2.41 us
    another operation x2 -> x0, other arithmetic: 1.36 us -> none
    reshape x1 -> x0, local copies, waits for them, and re-layouts: 1.33 us -> none  [shards(): jnp.concatenate([key_piece, value_piece], axis=1)]
    concatenate x1, other arithmetic: 1.08 us -> 0.08 us  [shards(): tag = jnp.concatenate([block_lists[0], block_counts]).astype(jnp.bfloat16)]
where the time goes in v4:
time: 78.4 us; the launch traced here: 78 us
  blocking collectives  46.8 us (60%)
  waiting for transfers between devices  14.1 us (18%)
  Pallas kernels  8.21 us (10%)
  starting transfers between devices  3.65 us (5%)
  local copies, waits for them, and re-layouts  2.41 us (3%)
  between operations  1.34 us (2%)
  other arithmetic  1.13 us (1%)
    all_to_all x1, blocking collectives, shards(): first_recv = lax.all_to_all(first_send, 'ctx', 0, 0, tiled=True)  17.4 us
    all_to_all x1, blocking collectives, shards(): lax.all_to_all(picked, 'ctx', 0, 0, tiled=True)  17.1 us
    all_to_all x1, waiting for transfers between devices, shards(): lax.all_to_all(pieces.reshape(peers, LIST * chunk_rows, both_width), 'ctx...  14.1 us
    all_to_all x1, blocking collectives, shards(): lax.all_to_all(summed, 'ctx', 0, 0, tiled=True)  12.2 us
    pallas_call x1, Pallas kernels, attend_all(): pl.pallas_call(attention_kernel(chunk_rows, heads_per_group, local_groups...  8.21 us
    all_to_all x1, starting transfers between devices, shards(): lax.all_to_all(pieces.reshape(peers, LIST * chunk_rows, both_width), 'ctx...  3.65 us
  transfers between devices with their start and end apart: 1, of which 1 were waited for; matrix products, arithmetic and copies ran while one was open for 0% of the time, Pallas kernels for 0%

profile of v4, /device:TPU:0, one launch (start us, length us, event | category | flops | bytes accessed | tf_op | source)
XLA Modules:
  0.0 78.0 jit_solution(13141665858579544311)
XLA Ops:
  1.3 0.0 copy-start
  1.3 0.6 copy-done
  1.9 0.1 fusion.7
  2.0 1.0 %maximum_maximum_fusion = bf16[8,16,1152]{2,1,0:T(8,128)(2,1)S(1)} fusion(bf16[8,16,512]{2,1,0:T(8,128)(2,1)} %bitcast.32, bf16[8,16,512]{2,1,0:T(8,128)(2,1)} %bitcast.33, bf16[1152]{0:T(1024)(128)(2,1)S(1)} %pad.7.clone), kind=kLoop, calls=%fused_computation.4 | loop fusion | flops 884736 | bytes 559360 | tf_op jit(solution)/shard_map/concatenate | solution.py:114
  3.0 17.4 %all_to_all.20 = bf16[8,16,1152]{2,1,0:T(8,128)(2,1)S(1)} all-to-all(bf16[8,16,1152]{2,1,0:T(8,128)(2,1)S(1)} %maximum_maximum_fusion), channel_id=1, replica_groups=mesh['parts'=2,'ctx'=8,'tp'=2] {'ctx'}, dimensions={0} | all-to-all | bytes 589824 | tf_op jit(solution)/shard_map/all_to_all | solution.py:117
  20.5 0.1 copy.37
  20.6 0.1 copy.32
  20.7 0.1 reshape.64
  20.8 0.6 gather_fusion
  21.4 17.1 %all_to_all.21 = bf16[8,32,1024]{2,1,0:T(8,128)(2,1)} all-to-all(bf16[8,32,1024]{2,1,0:T(8,128)(2,1)S(1)} %bitcast.29), channel_id=1, replica_groups=mesh['parts'=2,'ctx'=8,'tp'=2] {'ctx'}, dimensions={0} | all-to-all | bytes 1048576 | tf_op jit(solution)/shard_map/all_to_all | solution.py:126
  38.5 8.2 %shard_map.93 = (bf16[128,4096]{1,0:T(8,128)(2,1)}, bf16[128,4096]{1,0:T(8,128)(2,1)}, bf16[256,1024]{1,0:T(8,128)(2,1)}) custom-call(s32[1]{0:T(128)S(6)} %copy.42.count_ref, bf16[128,4096]{1,0:T(8,128)(2,1)} %q_ref.1, bf16[128,4096]{1,0:T(8,128)(2,1)} %do_ref.1, bf16[256,1024]{1,0:T(8,128)(2,1)} %bitcast.26, bf16[256,1024]{1,0:T(8,128)(2,1)} %bitcast.27), custom_call_target="tpu_custom_call" | custom-call | tf_op jit(solution)/shard_map/pallas_call | solution.py:79
  46.7 3.6 %all-to-all-start.2 = ((bf16[8,32,1024]{2,1,0:T(8,128)(2,1)}), bf16[8,32,1024]{2,1,0:T(8,128)(2,1)S(1)}, u32[]{:S(2)}, u32[]{:S(2)}) async-start(bf16[8,32,1024]{2,1,0:T(8,128)(2,1)} %bitcast.31), calls=%async_computation.2 | async-start | bytes 1048576 | tf_op jit(solution)/shard_map/all_to_all | solution.py:137
  50.4 14.1 %all-to-all-done.2 = bf16[8,32,1024]{2,1,0:T(8,128)(2,1)S(1)} async-done(((bf16[8,32,1024]{2,1,0:T(8,128)(2,1)}), bf16[8,32,1024]{2,1,0:T(8,128)(2,1)S(1)}, u32[]{:S(2)}, u32[]{:S(2)}) %all-to-all-start.2) | async-done | bytes 524320 | tf_op jit(solution)/shard_map/all_to_all | solution.py:137
  64.5 0.4 fusion
  64.9 0.2 copy.34
  65.1 12.2 %all_to_all.22 = bf16[8,16,1024]{2,1,0:T(8,128)(2,1)S(1)} all-to-all(bf16[8,16,1024]{2,1,0:T(8,128)(2,1)S(1)} %copy.34), channel_id=1, replica_groups=mesh['parts'=2,'ctx'=8,'tp'=2] {'ctx'}, dimensions={0} | all-to-all | bytes 524288 | tf_op jit(solution)/shard_map/all_to_all | solution.py:149
  77.3 0.7 slice_bitcast_fusion
  (10 shorter events, 0.1 us)
Async XLA Ops:
  1.3 0.7 copy-start
  46.7 17.8 %all-to-all-start.2 = ((bf16[8,32,1024]{2,1,0:T(8,128)(2,1)}), bf16[8,32,1024]{2,1,0:T(8,128)(2,1)S(1)}, u32[]{:S(2)}, u32[]{:S(2)}) async-start(bf16[8,32,1024]{2,1,0:T(8,128)(2,1)} %bitcast.31), calls=%async_computation.2 | async-start | bytes 1048576 | tf_op jit(solution)/shard_map/all_to_all | solution.py:137

commit v5 on v4

--- a/solution.py
+++ b/solution.py
@@ -10,21 +10,24 @@
 HEAD_SIZE = 128
 LIST = 2
 TAG_COLUMNS = 128
+GROUPS_PER_STEP = 4
 
 
-def attention_kernel(chunk_rows, heads_per_group, local_groups):
+def attention_kernel(chunk_rows, heads_per_group, local_groups, groups_per_step):
     score_scale = HEAD_SIZE ** (-0.5)
+    group_width = heads_per_group * HEAD_SIZE
 
-    def kernel(count_ref, q_ref, do_ref, k_ref, v_ref, o_ref, dq_ref, pieces_ref):
-        keys = k_ref[...]
-        values = v_ref[...]
-        key_total = keys.shape[0]
+    def one_group(live, q_ref, do_ref, k_ref, v_ref, o_ref, dq_ref, within):
+        key_cols = slice(within * HEAD_SIZE, (within + 1) * HEAD_SIZE)
+        keys = k_ref[:, key_cols]
+        values = v_ref[:, key_cols]
         query_rows = q_ref.shape[0]
-        slot = (lax.broadcasted_iota(jnp.int32, (1, key_total), 1) // chunk_rows) % LIST
-        live = slot < count_ref[0]
         nt = (((1,), (1,)), ((), ()))
         tn = (((0,), (0,)), ((), ()))
-        heads = [slice(a * HEAD_SIZE, (a + 1) * HEAD_SIZE) for a in range(heads_per_group)]
+        heads = [
+            slice(within * group_width + a * HEAD_SIZE, within * group_width + (a + 1) * HEAD_SIZE)
+            for a in range(heads_per_group)
+        ]
         q = jnp.concatenate([q_ref[:, cols] for cols in heads], axis=0)
         do = jnp.concatenate([do_ref[:, cols] for cols in heads], axis=0)
         scores = score_scale * lax.dot_general(q, keys, nt, preferred_element_type=jnp.float32)
@@ -53,32 +56,49 @@
         value_piece = lax.dot_general(
             weights_low, do, tn, preferred_element_type=jnp.float32
         ).astype(jnp.bfloat16)
-        group = pl.program_id(0)
-        for index in range(local_groups):
+        return key_piece, value_piece
 
-            @pl.when(group == index)
+    def kernel(count_ref, q_ref, do_ref, k_ref, v_ref, o_ref, dq_ref, pieces_ref):
+        key_total = k_ref.shape[0]
+        slot = (lax.broadcasted_iota(jnp.int32, (1, key_total), 1) // chunk_rows) % LIST
+        live = slot < count_ref[0]
+        pieces = [
+            one_group(live, q_ref, do_ref, k_ref, v_ref, o_ref, dq_ref, within)
+            for within in range(groups_per_step)
+        ]
+        step = pl.program_id(0)
+        for index in range(local_groups // groups_per_step):
+
+            @pl.when(step == index)
             def _():
-                key_cols = slice(index * HEAD_SIZE, (index + 1) * HEAD_SIZE)
-                value_cols = slice((local_groups + index) * HEAD_SIZE, (local_groups + index + 1) * HEAD_SIZE)
-                pieces_ref[:, key_cols] = key_piece
-                pieces_ref[:, value_cols] = value_piece
+                for within, (key_piece, value_piece) in enumerate(pieces):
+                    group = index * groups_per_step + within
+                    key_cols = slice(group * HEAD_SIZE, (group + 1) * HEAD_SIZE)
+                    value_cols = slice(
+                        (local_groups + group) * HEAD_SIZE, (local_groups + group + 1) * HEAD_SIZE
+                    )
+                    pieces_ref[:, key_cols] = key_piece
+                    pieces_ref[:, value_cols] = value_piece
 
     return kernel
 
 
-def attend_all(queries, output_gradient, fetched, count, chunk_rows):
+def attend_all(queries, output_gradient, fetched, count, chunk_rows, groups_per_step=GROUPS_PER_STEP):
     query_rows, query_width = queries.shape
     key_total, both_width = fetched.shape
     key_width = both_width // 2
     local_groups = key_width // HEAD_SIZE
+    groups_per_step = min(groups_per_step, local_groups)
+    steps = local_groups // groups_per_step
     heads_per_group = QUERY_HEADS // KEY_VALUE_HEADS
-    group_width = heads_per_group * HEAD_SIZE
-    row_block = pl.BlockSpec((query_rows, group_width), lambda g: (0, g))
-    key_block = pl.BlockSpec((key_total, HEAD_SIZE), lambda g: (0, g))
-    value_block = pl.BlockSpec((key_total, HEAD_SIZE), lambda g: (0, local_groups + g))
+    step_width = groups_per_step * heads_per_group * HEAD_SIZE
+    key_step = groups_per_step * HEAD_SIZE
+    row_block = pl.BlockSpec((query_rows, step_width), lambda i: (0, i))
+    key_block = pl.BlockSpec((key_total, key_step), lambda i: (0, i))
+    value_block = pl.BlockSpec((key_total, key_step), lambda i: (0, steps + i))
     return pl.pallas_call(
-        attention_kernel(chunk_rows, heads_per_group, local_groups),
-        grid=(local_groups,),
+        attention_kernel(chunk_rows, heads_per_group, local_groups, groups_per_step),
+        grid=(steps,),
         in_specs=[
             pl.BlockSpec(memory_space=pltpu.SMEM),
             row_block,
@@ -86,7 +106,7 @@
             key_block,
             value_block,
         ],
-        out_specs=[row_block, row_block, pl.BlockSpec((key_total, both_width), lambda g: (0, 0))],
+        out_specs=[row_block, row_block, pl.BlockSpec((key_total, both_width), lambda i: (0, 0))],
         out_shape=[
             jax.ShapeDtypeStruct((query_rows, query_width), jnp.bfloat16),
             jax.ShapeDtypeStruct((query_rows, query_width), jnp.bfloat16),

time: 78.4 us -> 77.4 us (0.987)
  Pallas kernels: 8.21 us -> 7.21 us
    pallas_call x1, Pallas kernels: 8.21 us -> 7.21 us  [attend_all(): pl.pallas_call(attention_kernel(chunk_rows, heads_per_group, local_groups...]
where the time goes in v5:
time: 77.4 us; the launch traced here: 77 us
  blocking collectives  46.8 us (60%)
  waiting for transfers between devices  14.1 us (18%)
  Pallas kernels  7.21 us (9%)
  starting transfers between devices  3.63 us (5%)
  local copies, waits for them, and re-layouts  2.41 us (3%)
  between operations  1.34 us (2%)
  other arithmetic  1.13 us (1%)
    all_to_all x1, blocking collectives, shards(): first_recv = lax.all_to_all(first_send, 'ctx', 0, 0, tiled=True)  17.4 us
    all_to_all x1, blocking collectives, shards(): lax.all_to_all(picked, 'ctx', 0, 0, tiled=True)  17.1 us
    all_to_all x1, waiting for transfers between devices, shards(): lax.all_to_all(pieces.reshape(peers, LIST * chunk_rows, both_width), 'ctx...  14.1 us
    all_to_all x1, blocking collectives, shards(): lax.all_to_all(summed, 'ctx', 0, 0, tiled=True)  12.2 us
    pallas_call x1, Pallas kernels, attend_all(): pl.pallas_call(attention_kernel(chunk_rows, heads_per_group, local_groups...  7.21 us
    all_to_all x1, starting transfers between devices, shards(): lax.all_to_all(pieces.reshape(peers, LIST * chunk_rows, both_width), 'ctx...  3.63 us
  transfers between devices with their start and end apart: 1, of which 1 were waited for; matrix products, arithmetic and copies ran while one was open for 0% of the time, Pallas kernels for 0%

profile of v5, /device:TPU:0, one launch (start us, length us, event | category | flops | bytes accessed | tf_op | source)
XLA Modules:
  0.0 77.0 jit_solution(16523106449359245828)
XLA Ops:
  1.3 0.0 copy-start
  1.3 0.6 copy-done
  1.9 0.1 fusion.7
  2.0 1.0 %maximum_maximum_fusion = bf16[8,16,1152]{2,1,0:T(8,128)(2,1)S(1)} fusion(bf16[8,16,512]{2,1,0:T(8,128)(2,1)} %bitcast.32, bf16[8,16,512]{2,1,0:T(8,128)(2,1)} %bitcast.33, bf16[1152]{0:T(1024)(128)(2,1)S(1)} %pad.7.clone), kind=kLoop, calls=%fused_computation.4 | loop fusion | flops 884736 | bytes 559360 | tf_op jit(solution)/shard_map/concatenate | solution.py:134
  3.0 17.4 %all_to_all.20 = bf16[8,16,1152]{2,1,0:T(8,128)(2,1)S(1)} all-to-all(bf16[8,16,1152]{2,1,0:T(8,128)(2,1)S(1)} %maximum_maximum_fusion), channel_id=1, replica_groups=mesh['parts'=2,'ctx'=8,'tp'=2] {'ctx'}, dimensions={0} | all-to-all | bytes 589824 | tf_op jit(solution)/shard_map/all_to_all | solution.py:137
  20.5 0.1 copy.37
  20.6 0.1 copy.32
  20.7 0.1 reshape.64
  20.8 0.6 gather_fusion
  21.4 17.1 %all_to_all.21 = bf16[8,32,1024]{2,1,0:T(8,128)(2,1)} all-to-all(bf16[8,32,1024]{2,1,0:T(8,128)(2,1)S(1)} %bitcast.29), channel_id=1, replica_groups=mesh['parts'=2,'ctx'=8,'tp'=2] {'ctx'}, dimensions={0} | all-to-all | bytes 1048576 | tf_op jit(solution)/shard_map/all_to_all | solution.py:146
  38.5 7.2 %shard_map.93 = (bf16[128,4096]{1,0:T(8,128)(2,1)}, bf16[128,4096]{1,0:T(8,128)(2,1)}, bf16[256,1024]{1,0:T(8,128)(2,1)}) custom-call(s32[1]{0:T(128)S(6)} %copy.42.count_ref, bf16[128,4096]{1,0:T(8,128)(2,1)} %q_ref.1, bf16[128,4096]{1,0:T(8,128)(2,1)} %do_ref.1, bf16[256,1024]{1,0:T(8,128)(2,1)} %bitcast.26, bf16[256,1024]{1,0:T(8,128)(2,1)} %bitcast.27), custom_call_target="tpu_custom_call" | custom-call | tf_op jit(solution)/shard_map/pallas_call | solution.py:99
  45.7 3.6 %all-to-all-start.2 = ((bf16[8,32,1024]{2,1,0:T(8,128)(2,1)}), bf16[8,32,1024]{2,1,0:T(8,128)(2,1)S(1)}, u32[]{:S(2)}, u32[]{:S(2)}) async-start(bf16[8,32,1024]{2,1,0:T(8,128)(2,1)} %bitcast.31), calls=%async_computation.2 | async-start | bytes 1048576 | tf_op jit(solution)/shard_map/all_to_all | solution.py:157
  49.4 14.1 %all-to-all-done.2 = bf16[8,32,1024]{2,1,0:T(8,128)(2,1)S(1)} async-done(((bf16[8,32,1024]{2,1,0:T(8,128)(2,1)}), bf16[8,32,1024]{2,1,0:T(8,128)(2,1)S(1)}, u32[]{:S(2)}, u32[]{:S(2)}) %all-to-all-start.2) | async-done | bytes 524320 | tf_op jit(solution)/shard_map/all_to_all | solution.py:157
  63.5 0.4 fusion
  63.9 0.2 copy.34
  64.0 12.2 %all_to_all.22 = bf16[8,16,1024]{2,1,0:T(8,128)(2,1)S(1)} all-to-all(bf16[8,16,1024]{2,1,0:T(8,128)(2,1)S(1)} %copy.34), channel_id=1, replica_groups=mesh['parts'=2,'ctx'=8,'tp'=2] {'ctx'}, dimensions={0} | all-to-all | bytes 524288 | tf_op jit(solution)/shard_map/all_to_all | solution.py:169
  76.3 0.7 slice_bitcast_fusion
  (10 shorter events, 0.1 us)
Async XLA Ops:
  1.3 0.7 copy-start
  45.7 17.7 %all-to-all-start.2 = ((bf16[8,32,1024]{2,1,0:T(8,128)(2,1)}), bf16[8,32,1024]{2,1,0:T(8,128)(2,1)S(1)}, u32[]{:S(2)}, u32[]{:S(2)}) async-start(bf16[8,32,1024]{2,1,0:T(8,128)(2,1)} %bitcast.31), calls=%async_computation.2 | async-start | bytes 1048576 | tf_op jit(solution)/shard_map/all_to_all | solution.py:157

commit v6 on v5

--- a/solution.py
+++ b/solution.py
@@ -115,6 +115,33 @@
     )(count, queries, output_gradient, fetched, fetched)
 
 
+def pack_kernel(list_ref, count_ref, k_ref, v_ref, out_ref):
+    key_width = k_ref.shape[1]
+    out_ref[:, :key_width] = k_ref[...]
+    out_ref[:, key_width : 2 * key_width] = v_ref[...]
+    lane = lax.broadcasted_iota(jnp.int32, (k_ref.shape[0], TAG_COLUMNS), 1)
+    tag = jnp.where(lane == 0, list_ref[0, 0], 0)
+    tag = jnp.where(lane == 1, list_ref[0, 1], tag)
+    tag = jnp.where(lane == LIST, count_ref[0], tag)
+    out_ref[:, 2 * key_width :] = tag.astype(jnp.float32).astype(jnp.bfloat16)
+
+
+def pack_rows(keys, values, block_lists, block_counts):
+    row_count, key_width = keys.shape
+    whole = lambda shape: pl.BlockSpec(shape, lambda: (0, 0))
+    return pl.pallas_call(
+        pack_kernel,
+        in_specs=[
+            pl.BlockSpec(memory_space=pltpu.SMEM),
+            pl.BlockSpec(memory_space=pltpu.SMEM),
+            whole((row_count, key_width)),
+            whole((row_count, key_width)),
+        ],
+        out_specs=whole((row_count, 2 * key_width + TAG_COLUMNS)),
+        out_shape=jax.ShapeDtypeStruct((row_count, 2 * key_width + TAG_COLUMNS), jnp.bfloat16),
+    )(block_lists, block_counts, keys, values)
+
+
 def make_shards(peers):
     def shards(
         queries, episode_key_cache, episode_value_cache, output_gradient, block_lists, block_counts
@@ -124,16 +151,12 @@
         both_width = 2 * key_width
         chunk_rows = row_count // peers
 
-        held = jnp.concatenate(
-            [episode_key_cache[:, 0, :], episode_value_cache[:, 0, :]], axis=1
-        )
-        tag = jnp.concatenate([block_lists[0], block_counts]).astype(jnp.bfloat16)
-        tag_block = jnp.broadcast_to(
-            jnp.pad(tag, (0, TAG_COLUMNS - LIST - 1)), (row_count, TAG_COLUMNS)
-        )
-        first_send = jnp.concatenate([held, tag_block], axis=1).reshape(
-            peers, chunk_rows, both_width + TAG_COLUMNS
-        )
+        first_send = pack_rows(
+            episode_key_cache.reshape(row_count, key_width),
+            episode_value_cache.reshape(row_count, key_width),
+            block_lists,
+            block_counts,
+        ).reshape(peers, chunk_rows, both_width + TAG_COLUMNS)
         first_recv = lax.all_to_all(first_send, "ctx", 0, 0, tiled=True)
         info = first_recv[:, 0, both_width : both_width + LIST + 1].astype(jnp.int32)
         lists_all = info[:, :LIST]

time: 77.4 us -> 77.6 us (level)
  Pallas kernels: 7.21 us -> 8.9 us
  other arithmetic: 1.13 us -> 0.02 us
    pallas_call x0 -> x1, Pallas kernels: none -> 1.71 us  [pack_rows(): pl.pallas_call(pack_kernel, in_specs=[pl.BlockSpec(memory_space=pltpu.SME...]
    concatenate x2 -> x0, other arithmetic: 1.1 us -> none  [the longest x1 1.02 us: shards(): jnp.concatenate([held, tag_block], axis=1)]
where the time goes in v6:
time: 77.6 us; the launch traced here: 77.1 us
  blocking collectives  47 us (61%)
  waiting for transfers between devices  14.1 us (18%)
  Pallas kernels  8.9 us (11%)
  starting transfers between devices  3.64 us (5%)
  local copies, waits for them, and re-layouts  1.76 us (2%)
  between operations  1.32 us (2%)
    all_to_all x1, blocking collectives, shards(): first_recv = lax.all_to_all(first_send, 'ctx', 0, 0, tiled=True)  17.6 us
    all_to_all x1, blocking collectives, shards(): lax.all_to_all(picked, 'ctx', 0, 0, tiled=True)  17.1 us
    all_to_all x1, waiting for transfers between devices, shards(): lax.all_to_all(pieces.reshape(peers, LIST * chunk_rows, both_width), 'ctx...  14.1 us
    all_to_all x1, blocking collectives, shards(): lax.all_to_all(summed, 'ctx', 0, 0, tiled=True)  12.2 us
    pallas_call x1, Pallas kernels, attend_all(): pl.pallas_call(attention_kernel(chunk_rows, heads_per_group, local_groups...  7.19 us
    all_to_all x1, starting transfers between devices, shards(): lax.all_to_all(pieces.reshape(peers, LIST * chunk_rows, both_width), 'ctx...  3.64 us
    pallas_call x1, Pallas kernels, pack_rows(): pl.pallas_call(pack_kernel, in_specs=[pl.BlockSpec(memory_space=pltpu.SME...  1.71 us
  transfers between devices with their start and end apart: 1, of which 1 were waited for; matrix products, arithmetic and copies ran while one was open for 0% of the time, Pallas kernels for 0%

profile of v6, /device:TPU:0, one launch (start us, length us, event | category | flops | bytes accessed | tf_op | source)
XLA Modules:
  0.0 77.1 jit_solution(7008393550360217521)
XLA Ops:
  1.3 1.7 %shard_map.93 = bf16[128,1152]{1,0:T(8,128)(2,1)} custom-call(s32[1,2]{1,0:T(1,128)} %list_ref.1, s32[1]{0:T(128)S(6)} %copy.36.count_ref, bf16[128,512]{1,0:T(8,128)(2,1)} %bitcast.32, bf16[128,512]{1,0:T(8,128)(2,1)} %bitcast.33), custom_call_target="tpu_custom_call" | custom-call | tf_op jit(solution)/shard_map/pallas_call | solution.py:132
  3.0 17.6 %all_to_all.20 = bf16[8,16,1152]{2,1,0:T(8,128)(2,1)S(1)} all-to-all(bf16[8,16,1152]{2,1,0:T(8,128)(2,1)} %bitcast.29), channel_id=1, replica_groups=mesh['parts'=2,'ctx'=8,'tp'=2] {'ctx'}, dimensions={0} | all-to-all | bytes 589824 | tf_op jit(solution)/shard_map/all_to_all | solution.py:160
  20.6 0.1 copy.31
  20.7 0.1 copy.26
  20.8 0.1 reshape.68
  20.9 0.6 gather_fusion
  21.5 17.1 %all_to_all.21 = bf16[8,32,1024]{2,1,0:T(8,128)(2,1)} all-to-all(bf16[8,32,1024]{2,1,0:T(8,128)(2,1)S(1)} %bitcast.28), channel_id=1, replica_groups=mesh['parts'=2,'ctx'=8,'tp'=2] {'ctx'}, dimensions={0} | all-to-all | bytes 1048576 | tf_op jit(solution)/shard_map/all_to_all | solution.py:169
  38.7 7.2 %shard_map.94 = (bf16[128,4096]{1,0:T(8,128)(2,1)}, bf16[128,4096]{1,0:T(8,128)(2,1)}, bf16[256,1024]{1,0:T(8,128)(2,1)}) custom-call(s32[1]{0:T(128)S(6)} %copy.36.count_ref, bf16[128,4096]{1,0:T(8,128)(2,1)} %q_ref.1, bf16[128,4096]{1,0:T(8,128)(2,1)} %do_ref.1, bf16[256,1024]{1,0:T(8,128)(2,1)} %bitcast.25, bf16[256,1024]{1,0:T(8,128)(2,1)} %bitcast.26), custom_call_target="tpu_custom_call" | custom-call | tf_op jit(solution)/shard_map/pallas_call | solution.py:99
  45.9 3.6 %all-to-all-start.2 = ((bf16[8,32,1024]{2,1,0:T(8,128)(2,1)}), bf16[8,32,1024]{2,1,0:T(8,128)(2,1)S(1)}, u32[]{:S(2)}, u32[]{:S(2)}) async-start(bf16[8,32,1024]{2,1,0:T(8,128)(2,1)} %bitcast.31), calls=%async_computation.2 | async-start | bytes 1048576 | tf_op jit(solution)/shard_map/all_to_all | solution.py:180
  49.5 14.1 %all-to-all-done.2 = bf16[8,32,1024]{2,1,0:T(8,128)(2,1)S(1)} async-done(((bf16[8,32,1024]{2,1,0:T(8,128)(2,1)}), bf16[8,32,1024]{2,1,0:T(8,128)(2,1)S(1)}, u32[]{:S(2)}, u32[]{:S(2)}) %all-to-all-start.2) | async-done | bytes 524320 | tf_op jit(solution)/shard_map/all_to_all | solution.py:180
  63.6 0.4 fusion
  64.0 0.2 copy.28
  64.2 12.2 %all_to_all.22 = bf16[8,16,1024]{2,1,0:T(8,128)(2,1)S(1)} all-to-all(bf16[8,16,1024]{2,1,0:T(8,128)(2,1)S(1)} %copy.28), channel_id=1, replica_groups=mesh['parts'=2,'ctx'=8,'tp'=2] {'ctx'}, dimensions={0} | all-to-all | bytes 524288 | tf_op jit(solution)/shard_map/all_to_all | solution.py:192
  76.4 0.7 slice_bitcast_fusion
  (8 shorter events, 0.1 us)
Async XLA Ops:
  45.9 17.7 %all-to-all-start.2 = ((bf16[8,32,1024]{2,1,0:T(8,128)(2,1)}), bf16[8,32,1024]{2,1,0:T(8,128)(2,1)S(1)}, u32[]{:S(2)}, u32[]{:S(2)}) async-start(bf16[8,32,1024]{2,1,0:T(8,128)(2,1)} %bitcast.31), calls=%async_computation.2 | async-start | bytes 1048576 | tf_op jit(solution)/shard_map/all_to_all | solution.py:180

commit v7 on v5

--- a/solution.py
+++ b/solution.py
@@ -13,7 +13,7 @@
 GROUPS_PER_STEP = 4
 
 
-def attention_kernel(chunk_rows, heads_per_group, local_groups, groups_per_step):
+def attention_kernel(chunk_rows, heads_per_group, local_groups, groups_per_step, pieces_only):
     score_scale = HEAD_SIZE ** (-0.5)
     group_width = heads_per_group * HEAD_SIZE
 
@@ -44,12 +44,14 @@
         )
         weight_grad = lax.dot_general(do, values, nt, preferred_element_type=jnp.float32)
         score_grad = (weights * (weight_grad - row_delta)).astype(jnp.bfloat16)
-        query_grad = (
-            score_scale * jnp.dot(score_grad, keys, preferred_element_type=jnp.float32)
-        ).astype(jnp.bfloat16)
-        for a, cols in enumerate(heads):
-            o_ref[:, cols] = attended[a * query_rows : (a + 1) * query_rows]
-            dq_ref[:, cols] = query_grad[a * query_rows : (a + 1) * query_rows]
+        if not pieces_only:
+            query_grad = (
+                score_scale * jnp.dot(score_grad, keys, preferred_element_type=jnp.float32)
+            ).astype(jnp.bfloat16)
+            for a, cols in enumerate(heads):
+                o_ref[:, cols] = attended[a * query_rows : (a + 1) * query_rows]
+                dq_ref[:, cols] = query_grad[a * query_rows : (a + 1) * query_rows]
+            return None
         key_piece = (
             score_scale * lax.dot_general(score_grad, q, tn, preferred_element_type=jnp.float32)
         ).astype(jnp.bfloat16)
@@ -58,14 +60,18 @@
         ).astype(jnp.bfloat16)
         return key_piece, value_piece
 
-    def kernel(count_ref, q_ref, do_ref, k_ref, v_ref, o_ref, dq_ref, pieces_ref):
+    def kernel(count_ref, q_ref, do_ref, k_ref, v_ref, *out_refs):
         key_total = k_ref.shape[0]
         slot = (lax.broadcasted_iota(jnp.int32, (1, key_total), 1) // chunk_rows) % LIST
         live = slot < count_ref[0]
+        o_ref, dq_ref = (None, None) if pieces_only else out_refs
         pieces = [
             one_group(live, q_ref, do_ref, k_ref, v_ref, o_ref, dq_ref, within)
             for within in range(groups_per_step)
         ]
+        if not pieces_only:
+            return
+        (pieces_ref,) = out_refs
         step = pl.program_id(0)
         for index in range(local_groups // groups_per_step):
 
@@ -96,23 +102,25 @@
     row_block = pl.BlockSpec((query_rows, step_width), lambda i: (0, i))
     key_block = pl.BlockSpec((key_total, key_step), lambda i: (0, i))
     value_block = pl.BlockSpec((key_total, key_step), lambda i: (0, steps + i))
-    return pl.pallas_call(
-        attention_kernel(chunk_rows, heads_per_group, local_groups, groups_per_step),
+    in_specs = [pl.BlockSpec(memory_space=pltpu.SMEM), row_block, row_block, key_block, value_block]
+    pieces = pl.pallas_call(
+        attention_kernel(chunk_rows, heads_per_group, local_groups, groups_per_step, True),
         grid=(steps,),
-        in_specs=[
-            pl.BlockSpec(memory_space=pltpu.SMEM),
-            row_block,
-            row_block,
-            key_block,
-            value_block,
-        ],
-        out_specs=[row_block, row_block, pl.BlockSpec((key_total, both_width), lambda i: (0, 0))],
+        in_specs=in_specs,
+        out_specs=pl.BlockSpec((key_total, both_width), lambda i: (0, 0)),
+        out_shape=jax.ShapeDtypeStruct((key_total, both_width), jnp.bfloat16),
+    )(count, queries, output_gradient, fetched, fetched)
+    attended, query_grad = pl.pallas_call(
+        attention_kernel(chunk_rows, heads_per_group, local_groups, groups_per_step, False),
+        grid=(steps,),
+        in_specs=in_specs,
+        out_specs=[row_block, row_block],
         out_shape=[
             jax.ShapeDtypeStruct((query_rows, query_width), jnp.bfloat16),
             jax.ShapeDtypeStruct((query_rows, query_width), jnp.bfloat16),
-            jax.ShapeDtypeStruct((key_total, both_width), jnp.bfloat16),
         ],
     )(count, queries, output_gradient, fetched, fetched)
+    return attended, query_grad, pieces
 
 
 def make_shards(peers):

time: 77.4 us -> 78.5 us (1.014)
  blocking collectives: 46.8 us -> 34.6 us
  Pallas kernels: 7.21 us -> 13.4 us
  starting transfers between devices: 3.63 us -> 7.28 us
  waiting for transfers between devices: 14.1 us -> 16.8 us
    all_to_all x1 -> x0, blocking collectives: 12.2 us -> none  [shards(): lax.all_to_all(summed, 'ctx', 0, 0, tiled=True)]
    pallas_call x1 -> x2, Pallas kernels: 7.21 us -> 13.4 us  [attend_all(): pl.pallas_call(attention_kernel(chunk_rows, heads_per_group, local_groups...]
    all_to_all x0 -> x1, starting transfers between devices: none -> 3.64 us  [shards(): lax.all_to_all(summed, 'ctx', 0, 0, tiled=True)]
    all_to_all x0 -> x1, waiting for transfers between devices: none -> 2.72 us  [shards(): lax.all_to_all(summed, 'ctx', 0, 0, tiled=True)]
  transfers between devices with their start and end apart: 1 -> 2, of which waited for: 1 -> 2; matrix products, arithmetic and copies ran while one was open for 0% -> 0% of each run, Pallas kernels for 0% -> 8%
where the time goes in v7:
time: 78.5 us; the launch traced here: 78 us
  blocking collectives  34.6 us (44%)
  waiting for transfers between devices  16.8 us (21%)
  Pallas kernels  13.4 us (17%)
  starting transfers between devices  7.28 us (9%)
  local copies, waits for them, and re-layouts  3.12 us (4%)
  between operations  1.33 us (2%)
  other arithmetic  1.13 us (1%)
    all_to_all x1, blocking collectives, shards(): first_recv = lax.all_to_all(first_send, 'ctx', 0, 0, tiled=True)  17.4 us
    all_to_all x1, blocking collectives, shards(): lax.all_to_all(picked, 'ctx', 0, 0, tiled=True)  17.1 us
    all_to_all x1, waiting for transfers between devices, shards(): lax.all_to_all(pieces.reshape(peers, LIST * chunk_rows, both_width), 'ctx...  14.1 us
    pallas_call x2, Pallas kernels, attend_all(): pl.pallas_call(attention_kernel(chunk_rows, heads_per_group, local_groups...  13.4 us
    all_to_all x1, starting transfers between devices, shards(): lax.all_to_all(summed, 'ctx', 0, 0, tiled=True)  3.64 us
    all_to_all x1, starting transfers between devices, shards(): lax.all_to_all(pieces.reshape(peers, LIST * chunk_rows, both_width), 'ctx...  3.63 us
    all_to_all x1, waiting for transfers between devices, shards(): lax.all_to_all(summed, 'ctx', 0, 0, tiled=True)  2.72 us
  transfers between devices with their start and end apart: 2, of which 2 were waited for; matrix products, arithmetic and copies ran while one was open for 0% of the time, Pallas kernels for 8%

profile of v7, /device:TPU:0, one launch (start us, length us, event | category | flops | bytes accessed | tf_op | source)
XLA Modules:
  0.0 78.0 jit_solution(11297914573752179492)
XLA Ops:
  1.3 0.0 copy-start
  1.3 0.6 copy-done
  1.9 0.1 fusion.7
  2.0 1.0 %maximum_maximum_fusion = bf16[8,16,1152]{2,1,0:T(8,128)(2,1)S(1)} fusion(bf16[8,16,512]{2,1,0:T(8,128)(2,1)} %bitcast.34, bf16[8,16,512]{2,1,0:T(8,128)(2,1)} %bitcast.35, bf16[1152]{0:T(1024)(128)(2,1)S(1)} %pad.7.clone), kind=kLoop, calls=%fused_computation.4 | loop fusion | flops 884736 | bytes 559360 | tf_op jit(solution)/shard_map/concatenate | solution.py:142
  3.0 17.4 %all_to_all.20 = bf16[8,16,1152]{2,1,0:T(8,128)(2,1)S(1)} all-to-all(bf16[8,16,1152]{2,1,0:T(8,128)(2,1)S(1)} %maximum_maximum_fusion), channel_id=1, replica_groups=mesh['parts'=2,'ctx'=8,'tp'=2] {'ctx'}, dimensions={0} | all-to-all | bytes 589824 | tf_op jit(solution)/shard_map/all_to_all | solution.py:145
  20.5 0.1 copy.37
  20.6 0.1 copy.32
  20.7 0.1 reshape.64
  20.8 0.6 gather_fusion
  21.4 17.1 %all_to_all.21 = bf16[8,32,1024]{2,1,0:T(8,128)(2,1)} all-to-all(bf16[8,32,1024]{2,1,0:T(8,128)(2,1)S(1)} %bitcast.31), channel_id=1, replica_groups=mesh['parts'=2,'ctx'=8,'tp'=2] {'ctx'}, dimensions={0} | all-to-all | bytes 1048576 | tf_op jit(solution)/shard_map/all_to_all | solution.py:154
  38.5 7.3 %shard_map.94 = bf16[256,1024]{1,0:T(8,128)(2,1)} custom-call(s32[1]{0:T(128)S(6)} %copy.42.count_ref, bf16[128,4096]{1,0:T(8,128)(2,1)} %q_ref.3, bf16[128,4096]{1,0:T(8,128)(2,1)} %do_ref.3, bf16[256,1024]{1,0:T(8,128)(2,1)} %bitcast.26, bf16[256,1024]{1,0:T(8,128)(2,1)} %bitcast.27), custom_call_target="tpu_custom_call" | custom-call | tf_op jit(solution)/shard_map/pallas_call | solution.py:106
  45.8 3.6 %all-to-all-start.2 = ((bf16[8,32,1024]{2,1,0:T(8,128)(2,1)}), bf16[8,32,1024]{2,1,0:T(8,128)(2,1)S(1)}, u32[]{:S(2)}, u32[]{:S(2)}) async-start(bf16[8,32,1024]{2,1,0:T(8,128)(2,1)} %bitcast.32), calls=%async_computation.2 | async-start | bytes 1048576 | tf_op jit(solution)/shard_map/all_to_all | solution.py:165
  49.5 14.1 %all-to-all-done.2 = bf16[8,32,1024]{2,1,0:T(8,128)(2,1)S(1)} async-done(((bf16[8,32,1024]{2,1,0:T(8,128)(2,1)}), bf16[8,32,1024]{2,1,0:T(8,128)(2,1)S(1)}, u32[]{:S(2)}, u32[]{:S(2)}) %all-to-all-start.2) | async-done | bytes 524320 | tf_op jit(solution)/shard_map/all_to_all | solution.py:165
  63.6 0.4 fusion
  64.0 0.9 %copy.34 = bf16[8,16,1024]{2,1,0:T(8,128)(2,1)} copy(bf16[8,16,1024]{2,0,1:T(8,128)(2,1)S(1)} %fusion) | data formatting | bytes 524288 | tf_op jit(solution)/shard_map/convert_element_type | solution.py:175
  64.8 3.6 %all-to-all-start.3 = ((bf16[8,16,1024]{2,1,0:T(8,128)(2,1)}), bf16[8,16,1024]{2,1,0:T(8,128)(2,1)S(1)}, u32[]{:S(2)}, u32[]{:S(2)}) async-start(bf16[8,16,1024]{2,1,0:T(8,128)(2,1)} %copy.34), calls=%async_computation.3 | async-start | bytes 524288 | tf_op jit(solution)/shard_map/all_to_all | solution.py:177
  68.5 6.1 %shard_map.93 = (bf16[128,4096]{1,0:T(8,128)(2,1)}, bf16[128,4096]{1,0:T(8,128)(2,1)}) custom-call(s32[1]{0:T(128)S(6)} %copy.42.count_ref, bf16[128,4096]{1,0:T(8,128)(2,1)} %q_ref.3, bf16[128,4096]{1,0:T(8,128)(2,1)} %do_ref.3, bf16[256,1024]{1,0:T(8,128)(2,1)} %bitcast.28, bf16[256,1024]{1,0:T(8,128)(2,1)} %bitcast.29), custom_call_target="tpu_custom_call" | custom-call | tf_op jit(solution)/shard_map/pallas_call | solution.py:113
  74.6 2.7 %all-to-all-done.3 = bf16[8,16,1024]{2,1,0:T(8,128)(2,1)S(1)} async-done(((bf16[8,16,1024]{2,1,0:T(8,128)(2,1)}), bf16[8,16,1024]{2,1,0:T(8,128)(2,1)S(1)}, u32[]{:S(2)}, u32[]{:S(2)}) %all-to-all-start.3) | async-done | bytes 262176 | tf_op jit(solution)/shard_map/all_to_all | solution.py:177
  77.3 0.7 slice_bitcast_fusion
  (10 shorter events, 0.1 us)
Async XLA Ops:
  1.3 0.7 copy-start
  45.8 17.7 %all-to-all-start.2 = ((bf16[8,32,1024]{2,1,0:T(8,128)(2,1)}), bf16[8,32,1024]{2,1,0:T(8,128)(2,1)S(1)}, u32[]{:S(2)}, u32[]{:S(2)}) async-start(bf16[8,32,1024]{2,1,0:T(8,128)(2,1)} %bitcast.32), calls=%async_computation.2 | async-start | bytes 1048576 | tf_op jit(solution)/shard_map/all_to_all | solution.py:165
  64.8 12.5 %all-to-all-start.3 = ((bf16[8,16,1024]{2,1,0:T(8,128)(2,1)}), bf16[8,16,1024]{2,1,0:T(8,128)(2,1)S(1)}, u32[]{:S(2)}, u32[]{:S(2)}) async-start(bf16[8,16,1024]{2,1,0:T(8,128)(2,1)} %copy.34), calls=%async_computation.3 | async-start | bytes 524288 | tf_op jit(solution)/shard_map/all_to_all | solution.py:177

commit v8 on v5

--- a/solution.py
+++ b/solution.py
@@ -127,11 +127,14 @@
         held = jnp.concatenate(
             [episode_key_cache[:, 0, :], episode_value_cache[:, 0, :]], axis=1
         )
-        tag = jnp.concatenate([block_lists[0], block_counts]).astype(jnp.bfloat16)
+        first_send, listed, counted = lax.optimization_barrier(
+            (jnp.pad(held, ((0, 0), (0, TAG_COLUMNS))), block_lists, block_counts)
+        )
+        tag = jnp.concatenate([listed[0], counted]).astype(jnp.bfloat16)
         tag_block = jnp.broadcast_to(
             jnp.pad(tag, (0, TAG_COLUMNS - LIST - 1)), (row_count, TAG_COLUMNS)
         )
-        first_send = jnp.concatenate([held, tag_block], axis=1).reshape(
+        first_send = lax.dynamic_update_slice(first_send, tag_block, (0, both_width)).reshape(
             peers, chunk_rows, both_width + TAG_COLUMNS
         )
         first_recv = lax.all_to_all(first_send, "ctx", 0, 0, tiled=True)

time: 77.4 us -> 76.7 us (level)
  no operation moved by 1% of the time
where the time goes in v8:
time: 76.7 us; the launch traced here: 76.4 us
  blocking collectives  46.8 us (61%)
  waiting for transfers between devices  14.1 us (18%)
  Pallas kernels  7.21 us (9%)
  starting transfers between devices  3.63 us (5%)
  local copies, waits for them, and re-layouts  1.78 us (2%)
  between operations  1.36 us (2%)
  other arithmetic  1.1 us (1%)
    all_to_all x1, blocking collectives, shards(): first_recv = lax.all_to_all(first_send, 'ctx', 0, 0, tiled=True)  17.4 us
    all_to_all x1, blocking collectives, shards(): lax.all_to_all(picked, 'ctx', 0, 0, tiled=True)  17.1 us
    all_to_all x1, waiting for transfers between devices, shards(): lax.all_to_all(pieces.reshape(peers, LIST * chunk_rows, both_width), 'ctx...  14.1 us
    all_to_all x1, blocking collectives, shards(): lax.all_to_all(summed, 'ctx', 0, 0, tiled=True)  12.2 us
    pallas_call x1, Pallas kernels, attend_all(): pl.pallas_call(attention_kernel(chunk_rows, heads_per_group, local_groups...  7.21 us
    all_to_all x1, starting transfers between devices, shards(): lax.all_to_all(pieces.reshape(peers, LIST * chunk_rows, both_width), 'ctx...  3.63 us
  transfers between devices with their start and end apart: 1, of which 1 were waited for; matrix products, arithmetic and copies ran while one was open for 0% of the time, Pallas kernels for 0%

profile of v8, /device:TPU:0, one launch (start us, length us, event | category | flops | bytes accessed | tf_op | source)
XLA Modules:
  0.0 76.4 jit_solution(6233576559368571395)
XLA Ops:
  1.3 0.0 copy-start
  1.3 1.0 %fusion.4 = bf16[128,1152]{1,0:T(8,128)(2,1)S(1)} fusion(bf16[128,512]{1,0:T(8,128)(2,1)} %bitcast.34, bf16[128,512]{1,0:T(8,128)(2,1)} %bitcast.35), kind=kLoop, calls=%fused_computation.7 | loop fusion | flops 1032192 | bytes 557056 | tf_op jit(solution)/shard_map/concatenate | solution.py:127
  2.3 0.0 copy-done
  2.3 0.1 fusion.10
  2.4 17.4 %all_to_all.20 = bf16[8,16,1152]{2,1,0:T(8,128)(2,1)S(1)} all-to-all(bf16[8,16,1152]{2,1,0:T(8,128)(2,1)S(1)} %bitcast.31), channel_id=1, replica_groups=mesh['parts'=2,'ctx'=8,'tp'=2] {'ctx'}, dimensions={0} | all-to-all | bytes 589824 | tf_op jit(solution)/shard_map/all_to_all | solution.py:140
  19.8 0.1 copy.35
  20.0 0.1 copy.30
  20.0 0.1 reshape.60
  20.2 0.6 gather_fusion
  20.8 17.1 %all_to_all.21 = bf16[8,32,1024]{2,1,0:T(8,128)(2,1)} all-to-all(bf16[8,32,1024]{2,1,0:T(8,128)(2,1)S(1)} %bitcast.30), channel_id=1, replica_groups=mesh['parts'=2,'ctx'=8,'tp'=2] {'ctx'}, dimensions={0} | all-to-all | bytes 1048576 | tf_op jit(solution)/shard_map/all_to_all | solution.py:149
  37.9 7.2 %shard_map.93 = (bf16[128,4096]{1,0:T(8,128)(2,1)}, bf16[128,4096]{1,0:T(8,128)(2,1)}, bf16[256,1024]{1,0:T(8,128)(2,1)}) custom-call(s32[1]{0:T(128)S(6)} %copy.41.count_ref, bf16[128,4096]{1,0:T(8,128)(2,1)} %q_ref.1, bf16[128,4096]{1,0:T(8,128)(2,1)} %do_ref.1, bf16[256,1024]{1,0:T(8,128)(2,1)} %bitcast.27, bf16[256,1024]{1,0:T(8,128)(2,1)} %bitcast.28), custom_call_target="tpu_custom_call" | custom-call | tf_op jit(solution)/shard_map/pallas_call | solution.py:99
  45.1 3.6 %all-to-all-start.2 = ((bf16[8,32,1024]{2,1,0:T(8,128)(2,1)}), bf16[8,32,1024]{2,1,0:T(8,128)(2,1)S(1)}, u32[]{:S(2)}, u32[]{:S(2)}) async-start(bf16[8,32,1024]{2,1,0:T(8,128)(2,1)} %bitcast.33), calls=%async_computation.2 | async-start | bytes 1048576 | tf_op jit(solution)/shard_map/all_to_all | solution.py:160
  48.8 14.1 %all-to-all-done.2 = bf16[8,32,1024]{2,1,0:T(8,128)(2,1)S(1)} async-done(((bf16[8,32,1024]{2,1,0:T(8,128)(2,1)}), bf16[8,32,1024]{2,1,0:T(8,128)(2,1)S(1)}, u32[]{:S(2)}, u32[]{:S(2)}) %all-to-all-start.2) | async-done | bytes 524320 | tf_op jit(solution)/shard_map/all_to_all | solution.py:160
  62.8 0.4 fusion
  63.2 0.2 copy.32
  63.4 12.2 %all_to_all.22 = bf16[8,16,1024]{2,1,0:T(8,128)(2,1)S(1)} all-to-all(bf16[8,16,1024]{2,1,0:T(8,128)(2,1)S(1)} %copy.32), channel_id=1, replica_groups=mesh['parts'=2,'ctx'=8,'tp'=2] {'ctx'}, dimensions={0} | all-to-all | bytes 524288 | tf_op jit(solution)/shard_map/all_to_all | solution.py:172
  75.7 0.7 slice_bitcast_fusion
  (10 shorter events, 0.1 us)
Async XLA Ops:
  1.3 1.0 %copy-start = (s32[1,2]{1,0:T(1,128)S(1)}, s32[1,2]{1,0:T(1,128)}, u32[]{:S(2)}) copy-start(s32[1,2]{1,0:T(1,128)} %param.10) | copy-start | bytes 28
  45.1 17.7 %all-to-all-start.2 = ((bf16[8,32,1024]{2,1,0:T(8,128)(2,1)}), bf16[8,32,1024]{2,1,0:T(8,128)(2,1)S(1)}, u32[]{:S(2)}, u32[]{:S(2)}) async-start(bf16[8,32,1024]{2,1,0:T(8,128)(2,1)} %bitcast.33), calls=%async_computation.2 | async-start | bytes 1048576 | tf_op jit(solution)/shard_map/all_to_all | solution.py:160

commit v9 on v8

--- a/solution.py
+++ b/solution.py
@@ -146,6 +146,12 @@
         picked = jnp.take(rows_held, lists_all, axis=0, mode="clip").reshape(
             peers, LIST * chunk_rows, both_width
         )
+        slot_live = jnp.arange(LIST, dtype=jnp.int32)[None, :] < counts_all[:, None]
+        selector = (
+            (lists_all[:, :, None] == jnp.arange(peers, dtype=jnp.int32)[None, None, :])
+            & slot_live[:, :, None]
+        ).astype(jnp.bfloat16)
+        picked, selector = lax.optimization_barrier((picked, selector))
         fetched = lax.all_to_all(picked, "ctx", 0, 0, tiled=True).reshape(
             LIST * row_count, both_width
         )
@@ -157,14 +163,10 @@
             chunk_rows,
         )
 
+        pieces, selector = lax.optimization_barrier((pieces, selector))
         back = lax.all_to_all(
             pieces.reshape(peers, LIST * chunk_rows, both_width), "ctx", 0, 0, tiled=True
         ).reshape(peers, LIST, chunk_rows, both_width)
-        slot_live = jnp.arange(LIST, dtype=jnp.int32)[None, :] < counts_all[:, None]
-        selector = (
-            (lists_all[:, :, None] == jnp.arange(peers, dtype=jnp.int32)[None, None, :])
-            & slot_live[:, :, None]
-        ).astype(jnp.bfloat16)
         summed = jnp.einsum(
             "qjrc,qjn->nrc", back, selector, preferred_element_type=jnp.float32
         ).astype(jnp.bfloat16)

time: 76.7 us -> 76.4 us (level)
  blocking collectives: 46.8 us -> 64.2 us
  waiting for transfers between devices: 14.1 us -> 0 us
  starting transfers between devices: 3.63 us -> 0 us
    all_to_all x0 -> x1, blocking collectives: none -> 17.7 us  [shards(): lax.all_to_all(pieces.reshape(peers, LIST * chunk_rows, both_width), 'ctx...]
    all_to_all x1 -> x0, waiting for transfers between devices: 14.1 us -> none  [shards(): lax.all_to_all(pieces.reshape(peers, LIST * chunk_rows, both_width), 'ctx...]
    all_to_all x1 -> x0, starting transfers between devices: 3.63 us -> none  [shards(): lax.all_to_all(pieces.reshape(peers, LIST * chunk_rows, both_width), 'ctx...]
  transfers between devices with their start and end apart: 1 -> 0, of which waited for: 1 -> 0; matrix products, arithmetic and copies ran while one was open for 0% -> 0% of each run, Pallas kernels for 0% -> 0%
where the time goes in v9:
time: 76.4 us; the launch traced here: 76.1 us
  blocking collectives  64.2 us (84%)
  Pallas kernels  7.21 us (9%)
  local copies, waits for them, and re-layouts  1.78 us (2%)
  between operations  1.36 us (2%)
  other arithmetic  1.11 us (1%)
    all_to_all x1, blocking collectives, shards(): lax.all_to_all(pieces.reshape(peers, LIST * chunk_rows, both_width), 'ctx...  17.7 us
    all_to_all x1, blocking collectives, shards(): first_recv = lax.all_to_all(first_send, 'ctx', 0, 0, tiled=True)  17.4 us
    all_to_all x1, blocking collectives, shards(): lax.all_to_all(picked, 'ctx', 0, 0, tiled=True)  17.1 us
    all_to_all x1, blocking collectives, shards(): lax.all_to_all(summed, 'ctx', 0, 0, tiled=True)  12 us
    pallas_call x1, Pallas kernels, attend_all(): pl.pallas_call(attention_kernel(chunk_rows, heads_per_group, local_groups...  7.21 us

profile of v9, /device:TPU:0, one launch (start us, length us, event | category | flops | bytes accessed | tf_op | source)
XLA Modules:
  0.0 76.1 jit_solution(14997968322118875681)
XLA Ops:
  1.3 0.0 copy-start
  1.3 1.0 %fusion.4 = bf16[128,1152]{1,0:T(8,128)(2,1)S(1)} fusion(bf16[128,512]{1,0:T(8,128)(2,1)} %bitcast.34, bf16[128,512]{1,0:T(8,128)(2,1)} %bitcast.35), kind=kLoop, calls=%fused_computation.7 | loop fusion | flops 1032192 | bytes 557056 | tf_op jit(solution)/shard_map/concatenate | solution.py:127
  2.3 0.0 copy-done
  2.3 0.1 fusion.8
  2.4 17.4 %all_to_all.20 = bf16[8,16,1152]{2,1,0:T(8,128)(2,1)S(1)} all-to-all(bf16[8,16,1152]{2,1,0:T(8,128)(2,1)S(1)} %bitcast.31), channel_id=1, replica_groups=mesh['parts'=2,'ctx'=8,'tp'=2] {'ctx'}, dimensions={0} | all-to-all | bytes 589824 | tf_op jit(solution)/shard_map/all_to_all | solution.py:140
  19.8 0.1 copy.35
  20.0 0.1 copy.30
  20.1 0.1 reshape.60
  20.2 0.6 gather_fusion
  20.8 17.1 %all_to_all.21 = bf16[8,32,1024]{2,1,0:T(8,128)(2,1)} all-to-all(bf16[8,32,1024]{2,1,0:T(8,128)(2,1)S(1)} %bitcast.29), channel_id=1, replica_groups=mesh['parts'=2,'ctx'=8,'tp'=2] {'ctx'}, dimensions={0} | all-to-all | bytes 1048576 | tf_op jit(solution)/shard_map/all_to_all | solution.py:155
  37.9 7.2 %shard_map.93 = (bf16[128,4096]{1,0:T(8,128)(2,1)}, bf16[128,4096]{1,0:T(8,128)(2,1)}, bf16[256,1024]{1,0:T(8,128)(2,1)}) custom-call(s32[1]{0:T(128)S(6)} %copy.41.count_ref, bf16[128,4096]{1,0:T(8,128)(2,1)} %q_ref.1, bf16[128,4096]{1,0:T(8,128)(2,1)} %do_ref.1, bf16[256,1024]{1,0:T(8,128)(2,1)} %bitcast.27, bf16[256,1024]{1,0:T(8,128)(2,1)} %bitcast.28), custom_call_target="tpu_custom_call" | custom-call | tf_op jit(solution)/shard_map/pallas_call | solution.py:99
  45.1 17.7 %all_to_all.22 = bf16[8,32,1024]{2,1,0:T(8,128)(2,1)S(1)} all-to-all(bf16[8,32,1024]{2,1,0:T(8,128)(2,1)} %bitcast.33), channel_id=1, replica_groups=mesh['parts'=2,'ctx'=8,'tp'=2] {'ctx'}, dimensions={0} | all-to-all | bytes 1048576 | tf_op jit(solution)/shard_map/all_to_all | solution.py:167
  62.8 0.4 fusion
  63.2 0.2 copy.32
  63.4 12.0 %all_to_all.23 = bf16[8,16,1024]{2,1,0:T(8,128)(2,1)S(1)} all-to-all(bf16[8,16,1024]{2,1,0:T(8,128)(2,1)S(1)} %copy.32), channel_id=1, replica_groups=mesh['parts'=2,'ctx'=8,'tp'=2] {'ctx'}, dimensions={0} | all-to-all | bytes 524288 | tf_op jit(solution)/shard_map/all_to_all | solution.py:174
  75.3 0.7 slice_bitcast_fusion
  (11 shorter events, 0.1 us)
Async XLA Ops:
  1.3 1.0 %copy-start = (s32[1,2]{1,0:T(1,128)S(1)}, s32[1,2]{1,0:T(1,128)}, u32[]{:S(2)}) copy-start(s32[1,2]{1,0:T(1,128)} %param.10) | copy-start | bytes 28

commit v10 on v9

--- a/solution.py
+++ b/solution.py
@@ -138,7 +138,7 @@
             peers, chunk_rows, both_width + TAG_COLUMNS
         )
         first_recv = lax.all_to_all(first_send, "ctx", 0, 0, tiled=True)
-        info = first_recv[:, 0, both_width : both_width + LIST + 1].astype(jnp.int32)
+        info = first_recv[:, 0, both_width:].astype(jnp.int32)
         lists_all = info[:, :LIST]
         counts_all = info[:, LIST]
 

time: 76.4 us -> 76.5 us (level)
  no operation moved by 1% of the time
where the time goes in v10:
time: 76.5 us; the launch traced here: 76.1 us
  blocking collectives  64.2 us (84%)
  Pallas kernels  7.22 us (9%)
  local copies, waits for them, and re-layouts  1.84 us (2%)
  between operations  1.36 us (2%)
  other arithmetic  1.1 us (1%)
    all_to_all x1, blocking collectives, shards(): lax.all_to_all(pieces.reshape(peers, LIST * chunk_rows, both_width), 'ctx...  17.7 us
    all_to_all x1, blocking collectives, shards(): first_recv = lax.all_to_all(first_send, 'ctx', 0, 0, tiled=True)  17.4 us
    all_to_all x1, blocking collectives, shards(): lax.all_to_all(picked, 'ctx', 0, 0, tiled=True)  17.1 us
    all_to_all x1, blocking collectives, shards(): lax.all_to_all(summed, 'ctx', 0, 0, tiled=True)  12 us
    pallas_call x1, Pallas kernels, attend_all(): pl.pallas_call(attention_kernel(chunk_rows, heads_per_group, local_groups...  7.22 us

profile of v10, /device:TPU:0, one launch (start us, length us, event | category | flops | bytes accessed | tf_op | source)
XLA Modules:
  0.0 76.1 jit_solution(7608611528520093885)
XLA Ops:
  1.3 0.0 copy-start
  1.3 1.0 %fusion.4 = bf16[128,1152]{1,0:T(8,128)(2,1)S(1)} fusion(bf16[128,512]{1,0:T(8,128)(2,1)} %bitcast.31, bf16[128,512]{1,0:T(8,128)(2,1)} %bitcast.32), kind=kLoop, calls=%fused_computation.7 | loop fusion | flops 1032192 | bytes 557056 | tf_op jit(solution)/shard_map/concatenate | solution.py:127
  2.3 0.0 copy-done
  2.3 0.1 fusion.8
  2.4 17.4 %all_to_all.20 = bf16[8,16,1152]{2,1,0:T(8,128)(2,1)S(1)} all-to-all(bf16[8,16,1152]{2,1,0:T(8,128)(2,1)S(1)} %bitcast.28), channel_id=1, replica_groups=mesh['parts'=2,'ctx'=8,'tp'=2] {'ctx'}, dimensions={0} | all-to-all | bytes 589824 | tf_op jit(solution)/shard_map/all_to_all | solution.py:140
  19.8 0.2 slice_reduce_fusion
  20.0 0.1 reshape.60
  20.1 0.1 copy.18
  20.2 0.6 gather_fusion
  20.8 17.1 %all_to_all.21 = bf16[8,32,1024]{2,1,0:T(8,128)(2,1)} all-to-all(bf16[8,32,1024]{2,1,0:T(8,128)(2,1)S(1)} %bitcast.26), channel_id=1, replica_groups=mesh['parts'=2,'ctx'=8,'tp'=2] {'ctx'}, dimensions={0} | all-to-all | bytes 1048576 | tf_op jit(solution)/shard_map/all_to_all | solution.py:155
  38.0 7.2 %shard_map.93 = (bf16[128,4096]{1,0:T(8,128)(2,1)}, bf16[128,4096]{1,0:T(8,128)(2,1)}, bf16[256,1024]{1,0:T(8,128)(2,1)}) custom-call(s32[1]{0:T(128)S(6)} %copy.25.count_ref, bf16[128,4096]{1,0:T(8,128)(2,1)} %q_ref.1, bf16[128,4096]{1,0:T(8,128)(2,1)} %do_ref.1, bf16[256,1024]{1,0:T(8,128)(2,1)} %bitcast.24, bf16[256,1024]{1,0:T(8,128)(2,1)} %bitcast.25), custom_call_target="tpu_custom_call" | custom-call | tf_op jit(solution)/shard_map/pallas_call | solution.py:99
  45.2 17.7 %all_to_all.22 = bf16[8,32,1024]{2,1,0:T(8,128)(2,1)S(1)} all-to-all(bf16[8,32,1024]{2,1,0:T(8,128)(2,1)} %bitcast.30), channel_id=1, replica_groups=mesh['parts'=2,'ctx'=8,'tp'=2] {'ctx'}, dimensions={0} | all-to-all | bytes 1048576 | tf_op jit(solution)/shard_map/all_to_all | solution.py:167
  62.9 0.4 fusion
  63.3 0.2 copy.20
  63.5 12.0 %all_to_all.23 = bf16[8,16,1024]{2,1,0:T(8,128)(2,1)S(1)} all-to-all(bf16[8,16,1024]{2,1,0:T(8,128)(2,1)S(1)} %copy.20), channel_id=1, replica_groups=mesh['parts'=2,'ctx'=8,'tp'=2] {'ctx'}, dimensions={0} | all-to-all | bytes 524288 | tf_op jit(solution)/shard_map/all_to_all | solution.py:174
  75.4 0.7 slice_bitcast_fusion
  (7 shorter events, 0.1 us)
Async XLA Ops:
  1.3 1.0 %copy-start = (s32[1,2]{1,0:T(1,128)S(1)}, s32[1,2]{1,0:T(1,128)}, u32[]{:S(2)}) copy-start(s32[1,2]{1,0:T(1,128)} %param.10) | copy-start | bytes 28

commit v11 on v10

--- a/solution.py
+++ b/solution.py
@@ -23,7 +23,6 @@
         values = v_ref[:, key_cols]
         query_rows = q_ref.shape[0]
         nt = (((1,), (1,)), ((), ()))
-        tn = (((0,), (0,)), ((), ()))
         heads = [
             slice(within * group_width + a * HEAD_SIZE, within * group_width + (a + 1) * HEAD_SIZE)
             for a in range(heads_per_group)
@@ -51,11 +50,11 @@
             o_ref[:, cols] = attended[a * query_rows : (a + 1) * query_rows]
             dq_ref[:, cols] = query_grad[a * query_rows : (a + 1) * query_rows]
         key_piece = (
-            score_scale * lax.dot_general(score_grad, q, tn, preferred_element_type=jnp.float32)
-        ).astype(jnp.bfloat16)
-        value_piece = lax.dot_general(
-            weights_low, do, tn, preferred_element_type=jnp.float32
-        ).astype(jnp.bfloat16)
+            score_scale * jnp.dot(q.T, score_grad, preferred_element_type=jnp.float32).T
+        ).astype(jnp.bfloat16)
+        value_piece = jnp.dot(do.T, weights_low, preferred_element_type=jnp.float32).T.astype(
+            jnp.bfloat16
+        )
         return key_piece, value_piece
 
     def kernel(count_ref, q_ref, do_ref, k_ref, v_ref, o_ref, dq_ref, pieces_ref):
@@ -168,7 +167,7 @@
             pieces.reshape(peers, LIST * chunk_rows, both_width), "ctx", 0, 0, tiled=True
         ).reshape(peers, LIST, chunk_rows, both_width)
         summed = jnp.einsum(
-            "qjrc,qjn->nrc", back, selector, preferred_element_type=jnp.float32
+            "qjn,qjrc->nrc", selector, back, preferred_element_type=jnp.float32
         ).astype(jnp.bfloat16)
 
         owned = lax.all_to_all(summed, "ctx", 0, 0, tiled=True).reshape(row_count, both_width)

time: 76.5 us -> 76.3 us (level)
  no operation moved by 1% of the time
where the time goes in v11:
time: 76.3 us; the launch traced here: 75.9 us
  blocking collectives  64.2 us (84%)
  Pallas kernels  7 us (9%)
  local copies, waits for them, and re-layouts  1.84 us (2%)
  between operations  1.36 us (2%)
  other arithmetic  1.1 us (1%)
    all_to_all x1, blocking collectives, shards(): lax.all_to_all(pieces.reshape(peers, LIST * chunk_rows, both_width), 'ctx...  17.7 us
    all_to_all x1, blocking collectives, shards(): first_recv = lax.all_to_all(first_send, 'ctx', 0, 0, tiled=True)  17.4 us
    all_to_all x1, blocking collectives, shards(): lax.all_to_all(picked, 'ctx', 0, 0, tiled=True)  17.1 us
    all_to_all x1, blocking collectives, shards(): lax.all_to_all(summed, 'ctx', 0, 0, tiled=True)  12 us
    pallas_call x1, Pallas kernels, attend_all(): pl.pallas_call(attention_kernel(chunk_rows, heads_per_group, local_groups...  7 us

profile of v11, /device:TPU:0, one launch (start us, length us, event | category | flops | bytes accessed | tf_op | source)
XLA Modules:
  0.0 75.9 jit_solution(3881340789914507139)
XLA Ops:
  1.3 0.0 copy-start
  1.3 1.0 %fusion.4 = bf16[128,1152]{1,0:T(8,128)(2,1)S(1)} fusion(bf16[128,512]{1,0:T(8,128)(2,1)} %bitcast.31, bf16[128,512]{1,0:T(8,128)(2,1)} %bitcast.32), kind=kLoop, calls=%fused_computation.7 | loop fusion | flops 1032192 | bytes 557056 | tf_op jit(solution)/shard_map/concatenate | solution.py:126
  2.3 0.0 copy-done
  2.3 0.1 fusion.8
  2.4 17.4 %all_to_all.20 = bf16[8,16,1152]{2,1,0:T(8,128)(2,1)S(1)} all-to-all(bf16[8,16,1152]{2,1,0:T(8,128)(2,1)S(1)} %bitcast.28), channel_id=1, replica_groups=mesh['parts'=2,'ctx'=8,'tp'=2] {'ctx'}, dimensions={0} | all-to-all | bytes 589824 | tf_op jit(solution)/shard_map/all_to_all | solution.py:139
  19.8 0.2 slice_reduce_fusion
  20.0 0.1 reshape.60
  20.1 0.1 copy.18
  20.2 0.6 gather_fusion
  20.8 17.1 %all_to_all.21 = bf16[8,32,1024]{2,1,0:T(8,128)(2,1)} all-to-all(bf16[8,32,1024]{2,1,0:T(8,128)(2,1)S(1)} %bitcast.26), channel_id=1, replica_groups=mesh['parts'=2,'ctx'=8,'tp'=2] {'ctx'}, dimensions={0} | all-to-all | bytes 1048576 | tf_op jit(solution)/shard_map/all_to_all | solution.py:154
  38.0 7.0 %shard_map.93 = (bf16[128,4096]{1,0:T(8,128)(2,1)}, bf16[128,4096]{1,0:T(8,128)(2,1)}, bf16[256,1024]{1,0:T(8,128)(2,1)}) custom-call(s32[1]{0:T(128)S(6)} %copy.25.count_ref, bf16[128,4096]{1,0:T(8,128)(2,1)} %q_ref.1, bf16[128,4096]{1,0:T(8,128)(2,1)} %do_ref.1, bf16[256,1024]{1,0:T(8,128)(2,1)} %bitcast.24, bf16[256,1024]{1,0:T(8,128)(2,1)} %bitcast.25), custom_call_target="tpu_custom_call" | custom-call | tf_op jit(solution)/shard_map/pallas_call | solution.py:98
  45.0 17.7 %all_to_all.22 = bf16[8,32,1024]{2,1,0:T(8,128)(2,1)S(1)} all-to-all(bf16[8,32,1024]{2,1,0:T(8,128)(2,1)} %bitcast.30), channel_id=1, replica_groups=mesh['parts'=2,'ctx'=8,'tp'=2] {'ctx'}, dimensions={0} | all-to-all | bytes 1048576 | tf_op jit(solution)/shard_map/all_to_all | solution.py:166
  62.7 0.4 fusion
  63.1 0.2 copy.20
  63.2 12.0 %all_to_all.23 = bf16[8,16,1024]{2,1,0:T(8,128)(2,1)S(1)} all-to-all(bf16[8,16,1024]{2,1,0:T(8,128)(2,1)S(1)} %copy.20), channel_id=1, replica_groups=mesh['parts'=2,'ctx'=8,'tp'=2] {'ctx'}, dimensions={0} | all-to-all | bytes 524288 | tf_op jit(solution)/shard_map/all_to_all | solution.py:173
  75.2 0.7 slice_bitcast_fusion
  (7 shorter events, 0.1 us)
Async XLA Ops:
  1.3 1.0 %copy-start = (s32[1,2]{1,0:T(1,128)S(1)}, s32[1,2]{1,0:T(1,128)}, u32[]{:S(2)}) copy-start(s32[1,2]{1,0:T(1,128)} %param.10) | copy-start | bytes 28

commit v12 on v11

--- a/solution.py
+++ b/solution.py
@@ -166,8 +166,9 @@
         back = lax.all_to_all(
             pieces.reshape(peers, LIST * chunk_rows, both_width), "ctx", 0, 0, tiled=True
         ).reshape(peers, LIST, chunk_rows, both_width)
-        summed = jnp.einsum(
-            "qjn,qjrc->nrc", selector, back, preferred_element_type=jnp.float32
+        summed = jnp.sum(
+            back.astype(jnp.float32)[None] * selector.astype(jnp.float32).transpose(2, 0, 1)[:, :, :, None, None],
+            axis=(1, 2),
         ).astype(jnp.bfloat16)
 
         owned = lax.all_to_all(summed, "ctx", 0, 0, tiled=True).reshape(row_count, both_width)

time: 76.3 us -> 77.9 us (1.021)
  blocking collectives: 64.2 us -> 46.8 us
  waiting for transfers between devices: 0 us -> 14.1 us
  starting transfers between devices: 0 us -> 3.63 us
  other arithmetic: 1.1 us -> 3.02 us
    all_to_all x1 -> x0, blocking collectives: 17.7 us -> none  [shards(): lax.all_to_all(pieces.reshape(peers, LIST * chunk_rows, both_width), 'ctx...]
    all_to_all x0 -> x1, waiting for transfers between devices: none -> 14.1 us  [shards(): lax.all_to_all(pieces.reshape(peers, LIST * chunk_rows, both_width), 'ctx...]
    all_to_all x0 -> x1, starting transfers between devices: none -> 3.63 us  [shards(): lax.all_to_all(pieces.reshape(peers, LIST * chunk_rows, both_width), 'ctx...]
    reduce_sum x0 -> x1, other arithmetic: none -> 1.08 us  [shards(): jnp.sum(back.astype(jnp.float32)[None] * selector.astype(jnp.float32).tra...]
  transfers between devices with their start and end apart: 0 -> 1, of which waited for: 0 -> 1; matrix products, arithmetic and copies ran while one was open for 0% -> 0% of each run, Pallas kernels for 0% -> 0%
where the time goes in v12:
time: 77.9 us; the launch traced here: 77.5 us
  blocking collectives  46.8 us (60%)
  waiting for transfers between devices  14.1 us (18%)
  Pallas kernels  7.01 us (9%)
  starting transfers between devices  3.63 us (5%)
  other arithmetic  3.02 us (4%)
  local copies, waits for them, and re-layouts  1.6 us (2%)
  between operations  1.34 us (2%)
    all_to_all x1, blocking collectives, shards(): first_recv = lax.all_to_all(first_send, 'ctx', 0, 0, tiled=True)  17.4 us
    all_to_all x1, blocking collectives, shards(): lax.all_to_all(picked, 'ctx', 0, 0, tiled=True)  17.1 us
    all_to_all x1, waiting for transfers between devices, shards(): lax.all_to_all(pieces.reshape(peers, LIST * chunk_rows, both_width), 'ctx...  14.1 us
    all_to_all x1, blocking collectives, shards(): lax.all_to_all(summed, 'ctx', 0, 0, tiled=True)  12.2 us
    pallas_call x1, Pallas kernels, attend_all(): pl.pallas_call(attention_kernel(chunk_rows, heads_per_group, local_groups...  7.01 us
    all_to_all x1, starting transfers between devices, shards(): lax.all_to_all(pieces.reshape(peers, LIST * chunk_rows, both_width), 'ctx...  3.63 us
  transfers between devices with their start and end apart: 1, of which 1 were waited for; matrix products, arithmetic and copies ran while one was open for 0% of the time, Pallas kernels for 0%

profile of v12, /device:TPU:0, one launch (start us, length us, event | category | flops | bytes accessed | tf_op | source)
XLA Modules:
  0.0 77.5 jit_solution(7319226884867503571)
XLA Ops:
  1.3 1.0 %fusion.2 = bf16[128,1152]{1,0:T(8,128)(2,1)S(1)} fusion(bf16[128,512]{1,0:T(8,128)(2,1)} %bitcast.26, bf16[128,512]{1,0:T(8,128)(2,1)} %bitcast.27), kind=kLoop, calls=%fused_computation.5 | loop fusion | flops 1032192 | bytes 557056 | tf_op jit(solution)/shard_map/concatenate | solution.py:126
  2.3 0.7 convert_bitcast_fusion.1
  2.9 0.1 fusion.5
  3.0 17.4 %all_to_all.20 = bf16[8,16,1152]{2,1,0:T(8,128)(2,1)S(1)} all-to-all(bf16[8,16,1152]{2,1,0:T(8,128)(2,1)S(1)} %bitcast.23), channel_id=1, replica_groups=mesh['parts'=2,'ctx'=8,'tp'=2] {'ctx'}, dimensions={0} | all-to-all | bytes 589824 | tf_op jit(solution)/shard_map/all_to_all | solution.py:139
  20.5 0.2 slice_reduce_fusion
  20.6 0.1 iota_compare_fusion.2
  20.7 0.1 reshape.66
  20.9 0.6 gather_fusion
  21.4 17.1 %all_to_all.21 = bf16[8,32,1024]{2,1,0:T(8,128)(2,1)} all-to-all(bf16[8,32,1024]{2,1,0:T(8,128)(2,1)S(1)} %bitcast.22), channel_id=1, replica_groups=mesh['parts'=2,'ctx'=8,'tp'=2] {'ctx'}, dimensions={0} | all-to-all | bytes 1048576 | tf_op jit(solution)/shard_map/all_to_all | solution.py:154
  38.6 7.0 %shard_map.93 = (bf16[128,4096]{1,0:T(8,128)(2,1)}, bf16[128,4096]{1,0:T(8,128)(2,1)}, bf16[256,1024]{1,0:T(8,128)(2,1)}) custom-call(s32[1]{0:T(128)S(6)} %copy.17.count_ref, bf16[128,4096]{1,0:T(8,128)(2,1)} %q_ref.1, bf16[128,4096]{1,0:T(8,128)(2,1)} %do_ref.1, bf16[256,1024]{1,0:T(8,128)(2,1)} %bitcast.20, bf16[256,1024]{1,0:T(8,128)(2,1)} %bitcast.21), custom_call_target="tpu_custom_call" | custom-call | tf_op jit(solution)/shard_map/pallas_call | solution.py:98
  45.6 3.6 %all-to-all-start.2 = ((bf16[8,32,1024]{2,1,0:T(8,128)(2,1)}), bf16[8,32,1024]{2,1,0:T(8,128)(2,1)S(1)}, u32[]{:S(2)}, u32[]{:S(2)}) async-start(bf16[8,32,1024]{2,1,0:T(8,128)(2,1)} %bitcast.25), calls=%async_computation.2 | async-start | bytes 1048576 | tf_op jit(solution)/shard_map/all_to_all | solution.py:166
  49.2 14.1 %all-to-all-done.2 = bf16[8,32,1024]{2,1,0:T(8,128)(2,1)S(1)} async-done(((bf16[8,32,1024]{2,1,0:T(8,128)(2,1)}), bf16[8,32,1024]{2,1,0:T(8,128)(2,1)S(1)}, u32[]{:S(2)}, u32[]{:S(2)}) %all-to-all-start.2) | async-done | bytes 524320 | tf_op jit(solution)/shard_map/all_to_all | solution.py:166
  63.3 0.1 bitcast_convert_fusion
  63.4 1.1 %multiply_reduce_fusion = bf16[8,16,1024]{2,1,0:T(8,128)(2,1)S(1)} fusion(f32[8,8,2]{2,1,0:T(8,128)S(1)} %convert_bitcast_fusion, f32[8,2,16,1024]{3,2,1,0:T(8,128)S(1)} %bitcast_convert_fusion), kind=kLoop, calls=%fused_computation.1 | loop fusion | flops 4063232 | bytes 1311232 | tf_op jit(solution)/shard_map/reduce_sum | solution.py:169
  64.5 12.2 %all_to_all.22 = bf16[8,16,1024]{2,1,0:T(8,128)(2,1)S(1)} all-to-all(bf16[8,16,1024]{2,1,0:T(8,128)(2,1)S(1)} %multiply_reduce_fusion), channel_id=1, replica_groups=mesh['parts'=2,'ctx'=8,'tp'=2] {'ctx'}, dimensions={0} | all-to-all | bytes 524288 | tf_op jit(solution)/shard_map/all_to_all | solution.py:174
  76.8 0.7 slice_bitcast_fusion
  (6 shorter events, 0.1 us)
Async XLA Ops:
  45.6 17.7 %all-to-all-start.2 = ((bf16[8,32,1024]{2,1,0:T(8,128)(2,1)}), bf16[8,32,1024]{2,1,0:T(8,128)(2,1)S(1)}, u32[]{:S(2)}, u32[]{:S(2)}) async-start(bf16[8,32,1024]{2,1,0:T(8,128)(2,1)} %bitcast.25), calls=%async_computation.2 | async-start | bytes 1048576 | tf_op jit(solution)/shard_map/all_to_all | solution.py:166
